TPU v7x, 1024 devices: a whole 8x8x8 slice. The times are simulated.
1024 devices in a mesh: ep: 64 (over y, z), et: 8 (over x_lo, core), rep: 2 (over x_hi).
Axes of the slice: x: 8 (x_hi: 2, x_lo: 4; x = x_hi * 4 + x_lo), y: 8, z: 8, core: 2. Of those that a mesh axis runs over, the one named last changes fastest.
Arguments:
- grad_out: bfloat16 [32768, 7168], P(('ep', 'rep'), 'et'), may hold values from -6 to 6
- combine: float32 [32768, 2], P(('ep', 'rep')), may hold values from 0.1 to 1
- routing: int32 [32768, 2], P(('ep', 'rep')), may hold values from 0 to 63, all different within a row; in each aligned block of 256 rows (0 to 255, 256 to 511, ...) at most 12 rows name the same one
- expert_down_matrix: bfloat16 [64, 7168, 1024], P('ep', 'et'), may hold values from -0.0625 to 0.0625
- gate_pre: bfloat16 [64, 2, 1024, 768], P('ep', 'rep', 'et'), may hold values from -6 to 6
- up_pre: bfloat16 [64, 2, 1024, 768], P('ep', 'rep', 'et'), may hold values from -6 to 6
Outputs:
- grad_gate: bfloat16 [64, 2, 1024, 768], P('ep', 'rep', 'et')
- up_projection_gradient: bfloat16 [64, 2, 1024, 768], P('ep', 'rep', 'et')
- grad_down: bfloat16 [64, 7168, 1024], P('ep', ('et', 'rep'))
Inputs may be any that keep to these rules, and one draw needn't show every extreme that they name: `routing`: each row names 2 different experts. Among the 256 rows of one token group (aligned blocks), no expert is named more than 12 times, a bound that some block reaches.
All inputs are finite; a program needn't handle non-finite values.
Results may differ from a plain program's by a relative error of at most 0.015.
Values may be sent and summed in bfloat16 or wider, within the bound.
No kernel may reach another device: no remote copies, remote signals or barrier semaphores. Data moves between devices by JAX's collectives and lax.ppermute only.
A program may use at most 32 MiB of HBM per device.

v0:
```python
import jax
import jax.numpy as jnp
from jax import lax
from jax.sharding import PartitionSpec as P


def local(grad_out, combine, routing, expert_down_matrix, gate_pre, up_pre):
    expert_count = lax.axis_size("ep")
    slot_count = gate_pre.shape[-1]
    capacity = slot_count // expert_count
    tok_rows, feat_cols = grad_out.shape
    pair_width = routing.shape[1]
    pair_total = tok_rows * pair_width
    targets = routing.reshape(pair_total)
    onehot = (targets[:, None] == jnp.arange(expert_count, dtype=jnp.int32)[None, :]).astype(
        jnp.int32
    )
    ranking = jnp.sum(
        (jnp.cumsum(onehot, axis=0, dtype=jnp.int32) - onehot) * onehot, axis=1, dtype=jnp.int32
    )
    destination = targets * capacity + ranking
    matches = destination[None, :] == jnp.arange(slot_count, dtype=jnp.int32)[:, None]
    filled = jnp.any(matches, axis=1)
    source_pair = jnp.sum(
        jnp.where(matches, jnp.arange(pair_total, dtype=jnp.int32)[None, :], 0),
        axis=1,
        dtype=jnp.int32,
    )
    weighted = (
        (grad_out.astype(jnp.float32)[:, None, :] * combine[:, :, None])
        .reshape(pair_total, feat_cols)
        .astype(jnp.bfloat16)
    )
    outgoing = jnp.where(
        filled[:, None], jnp.take(weighted, source_pair, axis=0), jnp.zeros((), jnp.bfloat16)
    )
    outgoing = outgoing.reshape(expert_count, capacity, feat_cols)
    incoming = lax.all_to_all(outgoing, "ep", split_axis=0, concat_axis=0, tiled=True).reshape(
        slot_count, feat_cols
    )
    weight_rows = expert_down_matrix[0]
    act_grad = lax.psum_scatter(
        lax.dot_general(
            weight_rows, incoming, (((0,), (1,)), ((), ())), preferred_element_type=jnp.float32
        ).astype(jnp.bfloat16),
        "et",
        scatter_dimension=0,
        tiled=True,
    ).astype(jnp.float32)
    gate_activation_values = gate_pre[0, 0].astype(jnp.float32)
    up_vals = up_pre[0, 0].astype(jnp.float32)
    gate_sig = jax.nn.sigmoid(gate_activation_values)
    grad_gate = (
        act_grad * up_vals * gate_sig * (1.0 + gate_activation_values * (1.0 - gate_sig))
    ).astype(jnp.bfloat16)
    up_projection_gradient = (act_grad * gate_activation_values * gate_sig).astype(jnp.bfloat16)
    activation = (gate_activation_values * gate_sig * up_vals).astype(jnp.bfloat16)
    partial_value_term = lax.dot_general(
        incoming,
        lax.all_gather(activation, "et", axis=0, tiled=True),
        (((0,), (1,)), ((), ())),
        preferred_element_type=jnp.float32,
    )
    summed = lax.psum_scatter(
        partial_value_term.astype(jnp.bfloat16), "rep", scatter_dimension=0, tiled=True
    )
    grad_down = summed[None]
    return (grad_gate[None, None], up_projection_gradient[None, None], grad_down)


def solution(mesh):
    return jax.shard_map(
        local,
        mesh=mesh,
        in_specs=(
            P(("ep", "rep"), "et"),
            P(("ep", "rep"), None),
            P(("ep", "rep"), None),
            P("ep", "et", None),
            P("ep", "rep", "et", None),
            P("ep", "rep", "et", None),
        ),
        out_specs=(
            P("ep", "rep", "et", None),
            P("ep", "rep", "et", None),
            P("ep", ("et", "rep"), None),
        ),
        check_vma=False,
    )
```

profile of v0, /device:TPU:64, one launch (start us, length us, event | category | flops | bytes accessed | tf_op | source)
XLA Modules:
  0.0 265.1 jit_solution(1412411680158841980)
XLA Ops:
  7.2 1.0 copy.29
  8.2 0.1 reshape.78
  8.4 0.1 eq.39
  8.5 1.2 reduce-window.6
  9.7 0.2 slice_reduce_fusion
  10.0 0.1 fusion.23
  10.1 0.2 fusion.5
  10.4 0.2 select_reduce_fusion
  10.9 0.8 copy.32
  11.7 0.1 mul.60
  11.9 1.7 mul.58
  13.6 3.4 %mul.59 = f32[512,896]{1,0:T(8,128)} reshape(f32[256,2,896]{2,1,0:T(2,128)} %mul.58) | data formatting | bytes 3670016 | tf_op jit(solution)/shard_map/mul | solution.py:30
  17.0 1.7 multiply_convert_fusion
  18.7 3.5 %gather_fusion = bf16[768,896]{1,0:T(8,128)(2,1)} fusion(bf16[512,896]{1,0:T(8,128)(2,1)S(1)} %multiply_convert_fusion, s32[1024]{0:T(1024)S(1)} %pad_clamp_fusion), kind=kCustom, calls=%fused_computation | custom fusion | bytes 2755584 | tf_op jit(solution)/shard_map/jit(_take)/gather | solution.py:35
  22.2 3.4 %gather.7 = bf16[64,12,896]{2,1,0:T(8,128)(2,1)} reshape(bf16[768,896]{1,0:T(8,128)(2,1)} %gather_fusion) | data formatting | bytes 2752512 | tf_op jit(solution)/shard_map/jit(_take)/gather | solution.py:35
  25.6 1.7 select_select_fusion
  27.4 66.8 %all_to_all.5 = bf16[64,12,896]{2,1,0:T(8,128)(2,1)} all-to-all(bf16[64,12,896]{2,1,0:T(8,128)(2,1)S(1)} %select_select_fusion), channel_id=1, replica_groups=mesh['ep'=64,'et'=8,'rep'=2] {'ep'}, dimensions={0} | all-to-all | bytes 2752512 | tf_op jit(solution)/shard_map/all_to_all | solution.py:38
  94.2 3.5 %reshape.80 = bf16[768,896]{1,0:T(8,128)(2,1)} reshape(bf16[64,12,896]{2,1,0:T(8,128)(2,1)} %all_to_all.5) | data formatting | bytes 2752512 | tf_op jit(solution)/shard_map/reshape | solution.py:38
  97.7 3.1 %fusion.6 = bf16[1024,768]{0,1:T(8,128)(2,1)S(1)} fusion(bf16[768,896]{1,0:T(8,128)(2,1)} %reshape.80, bf16[1,896,1024]{2,1,0:T(8,128)(2,1)S(1)} %copy-done), kind=kOutput, calls=%fused_computation.10 | convolution fusion | flops 1410072576 | bytes 4784128 | tf_op jit(solution)/shard_map/dot_general | solution.py:43
  100.8 1.6 copy.37
  102.5 0.8 copy-done.4
  103.3 0.8 copy.34
  104.1 1.7 copy.33
  105.9 41.6 %reduce-scatter.7.cloned.1.call-done = bf16[128,768]{1,0:T(8,128)(2,1)} async-done(((bf16[1024,768]{1,0:T(8,128)(2,1)}), bf16[128,768]{1,0:T(8,128)(2,1)}) %reduce-scatter.7.cloned.1.call-update) | async-done | bytes 196624
  147.4 1.7 copy.38
  149.2 2.1 fusion.12
  151.4 39.9 %all-gather.2.cloned.1.call-done = bf16[1024,768]{0,1:T(8,128)(2,1)} async-done(((bf16[128,768]{0,1:T(8,128)(2,1)}), bf16[1024,768]{0,1:T(8,128)(2,1)}) %all-gather.2.cloned.1.call-update) | async-done | bytes 1572880 | tf_op jit(solution)/shard_map/all_gather | solution.py:60
  191.2 4.3 %convolution_convert_fusion = bf16[896,1024]{1,0:T(8,128)(2,1)} fusion(bf16[768,896]{1,0:T(8,128)(2,1)S(1)} %copy-done.1, bf16[1024,768]{0,1:T(8,128)(2,1)} %all-gather.2.cloned.1.call-done), kind=kOutput, calls=%fused_computation.5 | convolution fusion | flops 1410203648 | bytes 4784128 | tf_op jit(solution)/shard_map/dot_general | solution.py:58
  195.6 0.9 copy-done.2
  196.5 0.8 copy.35
  197.3 0.8 copy.36
  198.1 60.4 %reduce-scatter.5.cloned.1.call-done = bf16[448,1024]{1,0:T(8,128)(2,1)} async-done(((bf16[896,1024]{1,0:T(8,128)(2,1)}), bf16[448,1024]{1,0:T(8,128)(2,1)}) %reduce-scatter.5.cloned.1.call-update) | async-done | bytes 917520 | tf_op jit(solution)/shard_map/reduce_scatter | solution.py:64
  (23 shorter events, 0.5 us)
Async XLA Ops:
  7.2 90.5 %copy-start = (bf16[1,896,1024]{2,1,0:T(8,128)(2,1)S(1)}, bf16[1,896,1024]{2,1,0:T(8,128)(2,1)}, u32[]{:S(2)}) copy-start(bf16[1,896,1024]{2,1,0:T(8,128)(2,1)} %param.9) | copy-start | bytes 5505028
  7.2 4.7 %copy-start.3 = (bf16[256,896]{1,0:T(8,128)(2,1)S(1)}, bf16[256,896]{1,0:T(8,128)(2,1)}, u32[]{:S(2)}) copy-start(bf16[256,896]{1,0:T(8,128)(2,1)} %param.6) | copy-start | bytes 1376260
  7.2 140.2 %reduce-scatter.7.cloned.1.call-start = ((), (), s32[]{:S(2)}) async-start(), calls=%async_computation.5 | async-start | bytes 1769472
  102.4 0.9 copy-start.4
  102.4 88.8 %copy-start.1 = (bf16[768,896]{1,0:T(8,128)(2,1)S(1)}, bf16[768,896]{1,0:T(8,128)(2,1)}, u32[]{:S(2)}) copy-start(bf16[768,896]{1,0:T(8,128)(2,1)} %reshape.80) | copy-start | bytes 4128772
  102.4 88.8 %all-gather.2.cloned.1.call-start = ((), (), s32[]{:S(2)}) async-start(), calls=%async_computation.3 | async-start | bytes 1769472 | tf_op jit(solution)/shard_map/all_gather | solution.py:60
  151.3 107.2 %reduce-scatter.5.cloned.1.call-start = ((), (), s32[]{:S(2)}) async-start(), calls=%async_computation.4 | async-start | bytes 2752512 | tf_op jit(solution)/shard_map/reduce_scatter | solution.py:64
  195.5 0.9 copy-start.2
Sparse Core Ops, SparseCore 0:
  102.5 44.8 reduce-scatter.6
  151.4 39.7 all-gather.1
  195.7 62.8 reduce-scatter.4
where the time goes:
time: 266 us; the launch traced here: 265 us
  waiting for transfers between devices  142 us (53%)
  blocking collectives  66.8 us (25%)
  local copies, waits for them, and re-layouts  27.5 us (10%)
  between operations  13.9 us (5%)
  matrix products  7.41 us (3%)
  other arithmetic  7.4 us (3%)
    all_to_all x1, blocking collectives, local(): lax.all_to_all(outgoing, 'ep', split_axis=0, concat_axis=0, tiled=True)  66.8 us
    reduce_scatter x1, waiting for transfers between devices, local(): lax.psum_scatter(partial_value_term.astype(jnp.bfloat16), 'rep', scatter_...  60.4 us
    unnamed x4, waiting for transfers between devices  41.6 us
    all_gather x1, waiting for transfers between devices, local(): lax.all_gather(activation, 'et', axis=0, tiled=True)  39.9 us
    unnamed x18, local copies, waits for them, and re-layouts  11.1 us
    gather x2, local copies, waits for them, and re-layouts, local(): jnp.take(weighted, source_pair, axis=0)  6.94 us
  transfers between devices with their start and end apart: 3, of which 3 were waited for; matrix products, arithmetic and copies ran while one was open for 2% of the time, Pallas kernels for 0%

commit v1 on v0

--- a/solution.py
+++ b/solution.py
@@ -6,11 +6,24 @@
 
 def local(grad_out, combine, routing, expert_down_matrix, gate_pre, up_pre):
     expert_count = lax.axis_size("ep")
+    rep_count = lax.axis_size("rep")
+    rep_index = lax.axis_index("rep")
     slot_count = gate_pre.shape[-1]
     capacity = slot_count // expert_count
     tok_rows, feat_cols = grad_out.shape
     pair_width = routing.shape[1]
     pair_total = tok_rows * pair_width
+
+    gate_activation_values = gate_pre[0, 0].astype(jnp.float32)
+    up_vals = up_pre[0, 0].astype(jnp.float32)
+    gate_sig = jax.nn.sigmoid(gate_activation_values)
+    activation = (gate_activation_values * gate_sig * up_vals).astype(jnp.bfloat16)
+    activation, gate_pre, up_pre = lax.optimization_barrier((activation, gate_pre, up_pre))
+    activation_all = lax.all_gather(activation, "et", axis=0, tiled=True)
+    gate_activation_values = gate_pre[0, 0].astype(jnp.float32)
+    up_vals = up_pre[0, 0].astype(jnp.float32)
+    gate_sig = jax.nn.sigmoid(gate_activation_values)
+
     targets = routing.reshape(pair_total)
     onehot = (targets[:, None] == jnp.arange(expert_count, dtype=jnp.int32)[None, :]).astype(
         jnp.int32
@@ -26,18 +39,26 @@
         axis=1,
         dtype=jnp.int32,
     )
-    weighted = (
-        (grad_out.astype(jnp.float32)[:, None, :] * combine[:, :, None])
-        .reshape(pair_total, feat_cols)
-        .astype(jnp.bfloat16)
-    )
+    pair_weight = jnp.take(combine.reshape(pair_total), source_pair, axis=0)
+    picked = jnp.take(grad_out, source_pair // pair_width, axis=0)
     outgoing = jnp.where(
-        filled[:, None], jnp.take(weighted, source_pair, axis=0), jnp.zeros((), jnp.bfloat16)
+        filled[:, None],
+        (picked.astype(jnp.float32) * pair_weight[:, None]).astype(jnp.bfloat16),
+        jnp.zeros((), jnp.bfloat16),
     )
     outgoing = outgoing.reshape(expert_count, capacity, feat_cols)
     incoming = lax.all_to_all(outgoing, "ep", split_axis=0, concat_axis=0, tiled=True).reshape(
         slot_count, feat_cols
     )
+
+    half = feat_cols // rep_count
+    away_rows = lax.dynamic_slice_in_dim(incoming, (1 - rep_index) * half, half, axis=1)
+    own_rows = lax.dynamic_slice_in_dim(incoming, rep_index * half, half, axis=1)
+    away_part = lax.dot_general(
+        away_rows, activation_all, (((0,), (1,)), ((), ())), preferred_element_type=jnp.float32
+    ).astype(jnp.bfloat16)
+    received = lax.ppermute(away_part, "rep", [(0, 1), (1, 0)])
+
     weight_rows = expert_down_matrix[0]
     act_grad = lax.psum_scatter(
         lax.dot_general(
@@ -47,25 +68,16 @@
         scatter_dimension=0,
         tiled=True,
     ).astype(jnp.float32)
-    gate_activation_values = gate_pre[0, 0].astype(jnp.float32)
-    up_vals = up_pre[0, 0].astype(jnp.float32)
-    gate_sig = jax.nn.sigmoid(gate_activation_values)
     grad_gate = (
         act_grad * up_vals * gate_sig * (1.0 + gate_activation_values * (1.0 - gate_sig))
     ).astype(jnp.bfloat16)
     up_projection_gradient = (act_grad * gate_activation_values * gate_sig).astype(jnp.bfloat16)
-    activation = (gate_activation_values * gate_sig * up_vals).astype(jnp.bfloat16)
-    partial_value_term = lax.dot_general(
-        incoming,
-        lax.all_gather(activation, "et", axis=0, tiled=True),
-        (((0,), (1,)), ((), ())),
-        preferred_element_type=jnp.float32,
-    )
-    summed = lax.psum_scatter(
-        partial_value_term.astype(jnp.bfloat16), "rep", scatter_dimension=0, tiled=True
-    )
-    grad_down = summed[None]
-    return (grad_gate[None, None], up_projection_gradient[None, None], grad_down)
+
+    own_part = lax.dot_general(
+        own_rows, activation_all, (((0,), (1,)), ((), ())), preferred_element_type=jnp.float32
+    ).astype(jnp.bfloat16)
+    grad_down = (own_part.astype(jnp.float32) + received.astype(jnp.float32)).astype(jnp.bfloat16)
+    return (grad_gate[None, None], up_projection_gradient[None, None], grad_down[None])
 
 
 def solution(mesh):

time: 266 us -> 188 us (0.71)
  the two profiles are of different devices: /device:TPU:64 before, /device:TPU:53 now
where the time goes in v1:
time: 188 us
  waiting for transfers between devices  102 us (54%)
  starting transfers between devices  28 us (15%)
  local copies, waits for them, and re-layouts  26.6 us (14%)
  between operations  14.3 us (8%)
  matrix products  10.1 us (5%)
  other arithmetic  6.89 us (4%)
    ppermute x1, waiting for transfers between devices, local(): received = lax.ppermute(away_part, 'rep', [(0, 1), (1, 0)])  54.9 us
    all_to_all x1, waiting for transfers between devices, local(): lax.all_to_all(outgoing, 'ep', split_axis=0, concat_axis=0, tiled=True)  46.8 us
    all_to_all x1, starting transfers between devices, local(): lax.all_to_all(outgoing, 'ep', split_axis=0, concat_axis=0, tiled=True)  22.6 us
    unnamed x22, local copies, waits for them, and re-layouts  7.7 us
    gather x2, local copies, waits for them, and re-layouts, local(): picked = jnp.take(grad_out, source_pair // pair_width, axis=0)  6.88 us
    ppermute x1, starting transfers between devices, local(): received = lax.ppermute(away_part, 'rep', [(0, 1), (1, 0)])  5.31 us
    gather x2, local copies, waits for them, and re-layouts, local(): pair_weight = jnp.take(combine.reshape(pair_total), source_pair, axis=0)  5.11 us
  transfers between devices with their start and end apart: 4, of which 2 were waited for; matrix products, arithmetic and copies ran while one was open for 10% of the time, Pallas kernels for 0%

profile of v1, /device:TPU:53, one launch (start us, length us, event | category | flops | bytes accessed | tf_op | source)
XLA Modules:
  0.0 187.6 jit_solution(7895978772539809494)
XLA Ops:
  7.2 0.9 copy.35
  8.1 0.1 eq.39
  8.3 0.1 reshape.154
  8.4 1.2 reduce-window.6
  9.6 0.2 slice_reduce_fusion
  10.1 0.2 select_reduce_fusion
  10.4 0.2 fusion.6
  10.7 0.8 copy.38
  11.5 0.1 reshape.156
  11.7 5.0 %gather_fusion.1 = f32[768]{0:T(1024)S(1)} fusion(f32[512]{0:T(512)S(1)} %reshape.156, s32[1024]{0:T(1024)S(1)} %get-tuple-element.25), kind=kCustom, calls=%fused_computation.1 | custom fusion | bytes 9216 | tf_op jit(solution)/shard_map/jit(_take)/gather | solution.py:42
  16.9 3.5 %gather_fusion = bf16[768,896]{1,0:T(8,128)(2,1)} fusion(bf16[256,896]{1,0:T(8,128)(2,1)S(1)} %copy-done.1, s32[1024]{0:T(1024)S(1)} %get-tuple-element.26), kind=kCustom, calls=%fused_computation | custom fusion | bytes 2755584 | tf_op jit(solution)/shard_map/jit(_take)/gather | solution.py:43
  20.4 3.4 %gather.13 = bf16[64,12,896]{2,1,0:T(8,128)(2,1)} reshape(bf16[768,896]{1,0:T(8,128)(2,1)} %gather_fusion) | data formatting | bytes 2752512 | tf_op jit(solution)/shard_map/jit(_take)/gather | solution.py:43
  23.9 3.0 %fusion = bf16[64,12,896]{2,1,0:T(8,128)(2,1)} fusion(f32[64,12]{1,0:T(8,128)S(1)} %and_select_fusion, bf16[64,12,896]{2,1,0:T(8,128)(2,1)} %gather.13, pred[64,12]{1,0:T(8,128)(4,1)S(1)} %compare_and_fusion, pred[64,12]{1,0:T(8,128)(4,1)S(1)} %broadcast_in_dim.57), kind=kLoop, calls=%fused_computation.3 | loop fusion | flops 3440640 | bytes 2757120 | tf_op jit(solution)/shard_map/jit(_where)/select_n | solution.py:44
  26.8 22.6 %all-to-all-start = ((bf16[64,12,896]{2,1,0:T(8,128)(2,1)}), bf16[64,12,896]{2,1,0:T(8,128)(2,1)}, u32[]{:S(2)}, u32[]{:S(2)}) async-start(bf16[64,12,896]{2,1,0:T(8,128)(2,1)} %fusion), calls=%async_computation | async-start | bytes 3670016 | tf_op jit(solution)/shard_map/all_to_all | solution.py:50
  49.5 0.2 copy.39
  49.7 0.2 copy.40
  49.9 0.8 fusion.26
  50.7 46.8 %all-to-all-done = bf16[64,12,896]{2,1,0:T(8,128)(2,1)} async-done(((bf16[64,12,896]{2,1,0:T(8,128)(2,1)}), bf16[64,12,896]{2,1,0:T(8,128)(2,1)}, u32[]{:S(2)}, u32[]{:S(2)}) %all-to-all-start) | async-done | bytes 1376288 | tf_op jit(solution)/shard_map/all_to_all | solution.py:50
  97.6 3.5 %reshape.157 = bf16[768,896]{1,0:T(8,128)(2,1)} reshape(bf16[64,12,896]{2,1,0:T(8,128)(2,1)} %all-to-all-done) | data formatting | bytes 2752512 | tf_op jit(solution)/shard_map/reshape | solution.py:50
  101.1 3.1 %fusion.7 = bf16[1024,768]{0,1:T(8,128)(2,1)S(1)} fusion(bf16[768,896]{1,0:T(8,128)(2,1)} %reshape.157, bf16[1,896,1024]{2,1,0:T(8,128)(2,1)S(1)} %copy-done), kind=kOutput, calls=%fused_computation.11 | convolution fusion | flops 1410072576 | bytes 4784128 | tf_op jit(solution)/shard_map/dot_general | solution.py:64
  104.2 1.6 copy.45
  105.9 1.3 copy-done.2
  107.1 3.4 %convolution_convert_fusion = bf16[448,1024]{1,0:T(8,128)(2,1)} fusion(bf16[1024,768]{0,1:T(8,128)(2,1)} %all-gather.2.cloned.1.call-done, bf16[768,896]{1,0:T(8,128)(2,1)S(1)} %copy-done.2, s32[]{:T(128)S(6)} %select_n.90), kind=kOutput, calls=%fused_computation.12 | convolution fusion | flops 705101824 | bytes 3276804 | tf_op jit(solution)/shard_map/dot_general | solution.py:57
  110.5 5.3 %collective-permute-start = (bf16[448,1024]{1,0:T(8,128)(2,1)}, bf16[448,1024]{1,0:T(8,128)(2,1)}, u32[]{:S(2)}, u32[]{:S(2)}) collective-permute-start(bf16[448,1024]{1,0:T(8,128)(2,1)} %convolution_convert_fusion), channel_id=1, source_target_pairs={{0,1},{1,0},{2,3},{3,2},{4,5},{5,4},{6,7},{7,6},{8,9},{9,8},{10,11... | collective-permute-start | bytes 2752520 | tf_op jit(solution)/shard_map/ppermute | solution.py:60
  115.8 0.8 copy.41
  116.6 1.7 copy.42
  118.4 54.9 %collective-permute-done = bf16[448,1024]{1,0:T(8,128)(2,1)} collective-permute-done((bf16[448,1024]{1,0:T(8,128)(2,1)}, bf16[448,1024]{1,0:T(8,128)(2,1)}, u32[]{:S(2)}, u32[]{:S(2)}) %collective-permute-start) | collective-permute-done | bytes 917536 | tf_op jit(solution)/shard_map/ppermute | solution.py:60
  173.2 3.6 %fusion.10 = bf16[1,448,1024]{2,1,0:T(8,128)(2,1)} fusion(bf16[448,1024]{1,0:T(8,128)(2,1)} %collective-permute-done, bf16[1024,768]{0,1:T(8,128)(2,1)} %all-gather.2.cloned.1.call-done, bf16[768,896]{1,0:T(8,128)(2,1)S(1)} %copy-done.2, s32[]{:T(128)S(6)} %select_n.89), kind=kOutput, calls=%fused_computation.14 | convolution fusion | flops 706936832 | bytes 4194308 | tf_op jit(solution)/shard_map/dot_general | solution.py:76
  176.8 1.1 copy.46
  177.9 1.2 fusion.27
  179.1 0.8 copy.43
  179.9 0.8 copy.44
  (31 shorter events, 0.8 us)
Async XLA Ops:
  7.2 93.9 %copy-start = (bf16[1,896,1024]{2,1,0:T(8,128)(2,1)S(1)}, bf16[1,896,1024]{2,1,0:T(8,128)(2,1)}, u32[]{:S(2)}) copy-start(bf16[1,896,1024]{2,1,0:T(8,128)(2,1)} %param.9) | copy-start | bytes 5505028
  11.7 5.2 %copy-start.1 = (bf16[256,896]{1,0:T(8,128)(2,1)S(1)}, bf16[256,896]{1,0:T(8,128)(2,1)}, u32[]{:S(2)}) copy-start(bf16[256,896]{1,0:T(8,128)(2,1)} %param.6) | copy-start | bytes 1376260
  26.8 22.7 %copy-start.5 = (bf16[1,1,128,768]{3,2,1,0:T(8,128)(2,1)S(1)}, bf16[1,1,128,768]{3,2,1,0:T(8,128)(2,1)}, u32[]{:S(2)}) copy-start(bf16[1,1,128,768]{3,2,1,0:T(8,128)(2,1)} %param.10) | copy-start | bytes 589828
  26.8 22.9 %copy-start.3 = (bf16[1,1,128,768]{3,2,1,0:T(8,128)(2,1)S(1)}, bf16[1,1,128,768]{3,2,1,0:T(8,128)(2,1)}, u32[]{:S(2)}) copy-start(bf16[1,1,128,768]{3,2,1,0:T(8,128)(2,1)} %param.11) | copy-start | bytes 589828
  26.8 70.7 %all-to-all-start = ((bf16[64,12,896]{2,1,0:T(8,128)(2,1)}), bf16[64,12,896]{2,1,0:T(8,128)(2,1)}, u32[]{:S(2)}, u32[]{:S(2)}) async-start(bf16[64,12,896]{2,1,0:T(8,128)(2,1)} %fusion), calls=%async_computation | async-start | bytes 3670016 | tf_op jit(solution)/shard_map/all_to_all | solution.py:50
  49.5 56.4 %all-gather.2.cloned.1.call-start = ((), (), s32[]{:S(2)}) async-start(), calls=%async_computation.2 | async-start | bytes 1769472 | tf_op jit(solution)/shard_map/all_gather | solution.py:22
  50.7 126.2 %reduce-scatter.4.cloned.1.call-start = ((), (), s32[]{:S(2)}) async-start(), calls=%async_computation.3 | async-start | bytes 1769472
  105.8 1.3 copy-start.2
  105.8 10.0 %copy-start.4 = (bf16[1,1,128,768]{3,2,1,0:T(8,128)(2,1)S(1)}, bf16[1,1,128,768]{3,2,1,0:T(8,128)(2,1)}, u32[]{:S(2)}) copy-start(bf16[1,1,128,768]{3,2,1,0:T(8,128)(2,1)} %param.11) | copy-start | bytes 589828
  110.5 62.7 %collective-permute-start = (bf16[448,1024]{1,0:T(8,128)(2,1)}, bf16[448,1024]{1,0:T(8,128)(2,1)}, u32[]{:S(2)}, u32[]{:S(2)}) collective-permute-start(bf16[448,1024]{1,0:T(8,128)(2,1)} %convolution_convert_fusion), channel_id=1, source_target_pairs={{0,1},{1,0},{2,3},{3,2},{4,5},{5,4},{6,7},{7,6},{8,9},{9,8},{10,11... | collective-permute-start | bytes 2752520 | tf_op jit(solution)/shard_map/ppermute | solution.py:60
  118.4 59.6 %copy-start.6 = (bf16[1,1,128,768]{2,3,1,0:T(8,128)(2,1)S(1)}, bf16[1,1,128,768]{2,3,1,0:T(8,128)(2,1)}, u32[]{:S(2)}) copy-start(bf16[1,1,128,768]{2,3,1,0:T(8,128)(2,1)} %copy.41) | copy-start | bytes 589828
Sparse Core Ops, SparseCore 0:
  53.4 41.8 all-gather.1
  105.9 58.9 reduce-scatter.3

commit v2 on v1

--- a/solution.py
+++ b/solution.py
@@ -33,37 +33,44 @@
     )
     destination = targets * capacity + ranking
     matches = destination[None, :] == jnp.arange(slot_count, dtype=jnp.int32)[:, None]
-    filled = jnp.any(matches, axis=1)
-    source_pair = jnp.sum(
-        jnp.where(matches, jnp.arange(pair_total, dtype=jnp.int32)[None, :], 0),
-        axis=1,
-        dtype=jnp.int32,
-    )
-    pair_weight = jnp.take(combine.reshape(pair_total), source_pair, axis=0)
-    picked = jnp.take(grad_out, source_pair // pair_width, axis=0)
-    outgoing = jnp.where(
-        filled[:, None],
-        (picked.astype(jnp.float32) * pair_weight[:, None]).astype(jnp.bfloat16),
-        jnp.zeros((), jnp.bfloat16),
-    )
-    outgoing = outgoing.reshape(expert_count, capacity, feat_cols)
-    incoming = lax.all_to_all(outgoing, "ep", split_axis=0, concat_axis=0, tiled=True).reshape(
-        slot_count, feat_cols
+    token_hit = jnp.any(matches.reshape(slot_count, tok_rows, pair_width), axis=2).astype(jnp.bfloat16)
+    pair_weight = jnp.sum(
+        jnp.where(matches, combine.reshape(pair_total)[None, :], 0.0), axis=1, dtype=jnp.float32
     )
 
+    def routed(cols):
+        picked = lax.dot_general(
+            token_hit, cols, (((1,), (0,)), ((), ())), preferred_element_type=jnp.float32
+        )
+        rows = (picked * pair_weight[:, None]).astype(jnp.bfloat16)
+        rows = rows.reshape(expert_count, capacity, cols.shape[1])
+        sent = lax.all_to_all(rows, "ep", split_axis=0, concat_axis=0, tiled=True)
+        return sent.reshape(slot_count, cols.shape[1])
+
     half = feat_cols // rep_count
-    away_rows = lax.dynamic_slice_in_dim(incoming, (1 - rep_index) * half, half, axis=1)
-    own_rows = lax.dynamic_slice_in_dim(incoming, rep_index * half, half, axis=1)
+    away_at = (1 - rep_index) * half
+    own_at = rep_index * half
+    away_rows = routed(lax.dynamic_slice_in_dim(grad_out, away_at, half, axis=1))
     away_part = lax.dot_general(
         away_rows, activation_all, (((0,), (1,)), ((), ())), preferred_element_type=jnp.float32
     ).astype(jnp.bfloat16)
     received = lax.ppermute(away_part, "rep", [(0, 1), (1, 0)])
+    own_rows = routed(lax.dynamic_slice_in_dim(grad_out, own_at, half, axis=1))
 
     weight_rows = expert_down_matrix[0]
+    block_sum = lax.dot_general(
+        lax.dynamic_slice_in_dim(weight_rows, away_at, half, axis=0),
+        away_rows,
+        (((0,), (1,)), ((), ())),
+        preferred_element_type=jnp.float32,
+    ) + lax.dot_general(
+        lax.dynamic_slice_in_dim(weight_rows, own_at, half, axis=0),
+        own_rows,
+        (((0,), (1,)), ((), ())),
+        preferred_element_type=jnp.float32,
+    )
     act_grad = lax.psum_scatter(
-        lax.dot_general(
-            weight_rows, incoming, (((0,), (1,)), ((), ())), preferred_element_type=jnp.float32
-        ).astype(jnp.bfloat16),
+        block_sum.astype(jnp.bfloat16),
         "et",
         scatter_dimension=0,
         tiled=True,

time: 188 us -> 182 us (0.968)
  the two profiles are of different devices: /device:TPU:53 before, /device:TPU:56 now
where the time goes in v2:
time: 182 us; the launch traced here: 181 us
  waiting for transfers between devices  108 us (59%)
  starting transfers between devices  31.9 us (18%)
  between operations  14.3 us (8%)
  local copies, waits for them, and re-layouts  11.5 us (6%)
  matrix products  11.1 us (6%)
  other arithmetic  4.59 us (3%)
    ppermute x1, waiting for transfers between devices, local(): received = lax.ppermute(away_part, 'rep', [(0, 1), (1, 0)])  57.8 us
    all_to_all x2, waiting for transfers between devices, routed(): sent = lax.all_to_all(rows, 'ep', split_axis=0, concat_axis=0, tiled=True)  49.9 us
    all_to_all x2, starting transfers between devices, routed(): sent = lax.all_to_all(rows, 'ep', split_axis=0, concat_axis=0, tiled=True)  29.4 us
  transfers between devices with their start and end apart: 5, of which 3 were waited for; matrix products, arithmetic and copies ran while one was open for 10% of the time, Pallas kernels for 0%

profile of v2, /device:TPU:56, one launch (start us, length us, event | category | flops | bytes accessed | tf_op | source)
XLA Modules:
  0.0 181.1 jit_solution(7094385456263171465)
XLA Ops:
  7.2 1.0 copy.27
  8.2 0.1 eq.49
  8.3 0.1 eq.45
  8.5 1.2 reduce-window.6
  9.7 0.2 slice_reduce_fusion
  10.0 0.1 fusion.29
  10.1 0.1 reduce_sum.21
  10.2 0.8 copy.31
  11.1 0.1 broadcast_in_dim.28
  11.2 0.1 copy.30
  11.3 0.3 fusion
  11.6 0.2 select_reduce_fusion
  11.8 0.6 fusion.1
  12.4 0.3 copy.32
  12.7 1.2 reshape.67
  14.0 22.9 %all-to-all-start = ((bf16[64,12,448]{2,1,0:T(8,128)(2,1)}), bf16[64,12,448]{2,1,0:T(8,128)(2,1)S(1)}, u32[]{:S(2)}, u32[]{:S(2)}) async-start(bf16[64,12,448]{2,1,0:T(8,128)(2,1)} %reshape.67), calls=%async_computation | async-start | bytes 2097152 | tf_op jit(solution)/shard_map/all_to_all | solution.py:47
  36.9 0.8 fusion.22
  37.7 2.4 %fusion.2 = bf16[768,448]{0,1:T(8,128)(2,1)} fusion(pred[768,256]{1,0:T(8,128)(4,1)S(1)} %fusion, f32[768]{0:T(1024)S(1)} %select_reduce_fusion, bf16[256,896]{1,0:T(8,128)(2,1)} %param.6, s32[]{:T(128)S(6)} %select_n.14), kind=kOutput, calls=%fused_computation.11 | convolution fusion | flops 176848896 | bytes 1149956 | tf_op jit(solution)/shard_map/dot_general | solution.py:42
  40.1 2.3 %copy.33 = bf16[768,448]{1,0:T(8,128)(2,1)} copy(bf16[768,448]{0,1:T(8,128)(2,1)} %fusion.2) | data formatting | bytes 1376256 | tf_op jit(solution)/shard_map/convert_element_type | solution.py:45
  42.4 2.3 %reshape.69 = bf16[64,12,448]{2,1,0:T(8,128)(2,1)} reshape(bf16[768,448]{1,0:T(8,128)(2,1)} %copy.33) | data formatting | bytes 1376256 | tf_op jit(solution)/shard_map/reshape | solution.py:46
  44.6 21.9 %all-to-all-done = bf16[64,12,448]{2,1,0:T(8,128)(2,1)S(1)} async-done(((bf16[64,12,448]{2,1,0:T(8,128)(2,1)}), bf16[64,12,448]{2,1,0:T(8,128)(2,1)S(1)}, u32[]{:S(2)}, u32[]{:S(2)}) %all-to-all-start) | async-done | bytes 688160 | tf_op jit(solution)/shard_map/all_to_all | solution.py:47
  66.5 6.5 %all-to-all-start.1 = ((bf16[64,12,448]{2,1,0:T(8,128)(2,1)}), bf16[64,12,448]{2,1,0:T(8,128)(2,1)}, u32[]{:S(2)}, u32[]{:S(2)}) async-start(bf16[64,12,448]{2,1,0:T(8,128)(2,1)} %reshape.69), calls=%async_computation.1 | async-start | bytes 2097152 | tf_op jit(solution)/shard_map/all_to_all | solution.py:47
  73.1 1.3 reshape.68
  74.4 28.0 %all-to-all-done.1 = bf16[64,12,448]{2,1,0:T(8,128)(2,1)} async-done(((bf16[64,12,448]{2,1,0:T(8,128)(2,1)}), bf16[64,12,448]{2,1,0:T(8,128)(2,1)}, u32[]{:S(2)}, u32[]{:S(2)}) %all-to-all-start.1) | async-done | bytes 688160 | tf_op jit(solution)/shard_map/all_to_all | solution.py:47
  102.4 1.5 reshape.70
  104.0 1.1 fusion.5
  105.0 2.3 %add_convert_fusion = bf16[1024,768]{1,0:T(8,128)(2,1)} fusion(f32[1024,768]{1,0:T(8,128)S(1)} %fusion.5, bf16[768,448]{1,0:T(8,128)(2,1)S(1)} %reshape.70, bf16[1,896,1024]{2,1,0:T(8,128)(2,1)S(1)} %copy-done, s32[]{:T(128)S(6)} %select_n.14), kind=kOutput, calls=%fused_computation | convolution fusion | flops 706215936 | bytes 6422532 | tf_op jit(solution)/shard_map/dot_general | solution.py:66
  107.4 2.7 %convolution_convert_fusion = bf16[448,1024]{1,0:T(8,128)(2,1)S(1)} fusion(bf16[768,448]{1,0:T(8,128)(2,1)S(1)} %copy-done.1, bf16[1024,768]{1,0:T(8,128)(2,1)} %all-gather.2.cloned.1.call-done), kind=kOutput, calls=%fused_computation.6 | convolution fusion | flops 705101824 | bytes 3178496 | tf_op jit(solution)/shard_map/dot_general | solution.py:54
  110.1 2.4 %collective-permute-start = (bf16[448,1024]{1,0:T(8,128)(2,1)S(1)}, bf16[448,1024]{1,0:T(8,128)(2,1)S(1)}, u32[]{:S(2)}, u32[]{:S(2)}) collective-permute-start(bf16[448,1024]{1,0:T(8,128)(2,1)S(1)} %convolution_convert_fusion), channel_id=1, source_target_pairs={{0,1},{1,0},{2,3},{3,2},{4,5},{5,4},{6,7},{7,6},{8,9},{9,8},{10,11... | collective-permute-start | bytes 2752520 | tf_op jit(solution)/shard_map/ppermute | solution.py:57
  112.5 57.8 %collective-permute-done = bf16[448,1024]{1,0:T(8,128)(2,1)S(1)} collective-permute-done((bf16[448,1024]{1,0:T(8,128)(2,1)S(1)}, bf16[448,1024]{1,0:T(8,128)(2,1)S(1)}, u32[]{:S(2)}, u32[]{:S(2)}) %collective-permute-start) | collective-permute-done | bytes 917536 | tf_op jit(solution)/shard_map/ppermute | solution.py:57
  170.3 2.1 %fusion.3 = bf16[1,448,1024]{2,1,0:T(8,128)(2,1)} fusion(bf16[448,1024]{1,0:T(8,128)(2,1)S(1)} %collective-permute-done, bf16[768,448]{1,0:T(8,128)(2,1)S(1)} %reshape.70, bf16[1024,768]{1,0:T(8,128)(2,1)S(1)} %copy-done.7), kind=kOutput, calls=%fused_computation.12 | convolution fusion | flops 706936832 | bytes 4096000 | tf_op jit(solution)/shard_map/dot_general | solution.py:83
  172.4 1.9 %fusion.25 = (bf16[1,1,128,768]{3,2,1,0:T(8,128)(2,1)}, bf16[1,1,128,768]{3,2,1,0:T(8,128)(2,1)}) fusion(bf16[1,1,128,768]{3,2,1,0:T(8,128)(2,1)S(1)} %copy-done.3, bf16[128,768]{1,0:T(8,128)(2,1)} %reduce-scatter.2.cloned.1.call-done, bf16[1,1,128,768]{3,2,1,0:T(8,128)(2,1)S(1)} %copy-done.5), kind=kLoop, calls=%fused_computation.40 | loop fusion | flops 1572864 | bytes 983040 | tf_op jit(solution)/shard_map/broadcast_in_dim | solution.py:87
  (29 shorter events, 0.3 us)
Async XLA Ops:
  7.2 96.8 %copy-start = (bf16[1,896,1024]{2,1,0:T(8,128)(2,1)S(1)}, bf16[1,896,1024]{2,1,0:T(8,128)(2,1)}, u32[]{:S(2)}) copy-start(bf16[1,896,1024]{2,1,0:T(8,128)(2,1)} %param.9) | copy-start | bytes 5505028
  7.2 4.1 %copy-start.6 = (s32[256,2]{0,1:T(2,128)S(1)}, s32[256,2]{0,1:T(2,128)}, u32[]{:S(2)}) copy-start(s32[256,2]{0,1:T(2,128)} %param.8) | copy-start | bytes 6148
  7.2 4.6 %copy-start.8 = (bf16[256,896]{1,0:T(8,128)(2,1)S(1)}, bf16[256,896]{1,0:T(8,128)(2,1)}, u32[]{:S(2)}) copy-start(bf16[256,896]{1,0:T(8,128)(2,1)} %param.6) | copy-start | bytes 1376260
  12.7 24.2 %copy-start.2 = (bf16[1,1,128,768]{3,2,1,0:T(8,128)(2,1)S(1)}, bf16[1,1,128,768]{3,2,1,0:T(8,128)(2,1)}, u32[]{:S(2)}) copy-start(bf16[1,1,128,768]{3,2,1,0:T(8,128)(2,1)} %param.10) | copy-start | bytes 589828
  12.7 24.2 %copy-start.4 = (bf16[1,1,128,768]{3,2,1,0:T(8,128)(2,1)S(1)}, bf16[1,1,128,768]{3,2,1,0:T(8,128)(2,1)}, u32[]{:S(2)}) copy-start(bf16[1,1,128,768]{3,2,1,0:T(8,128)(2,1)} %param.11) | copy-start | bytes 589828
  14.0 52.6 %all-to-all-start = ((bf16[64,12,448]{2,1,0:T(8,128)(2,1)}), bf16[64,12,448]{2,1,0:T(8,128)(2,1)S(1)}, u32[]{:S(2)}, u32[]{:S(2)}) async-start(bf16[64,12,448]{2,1,0:T(8,128)(2,1)} %reshape.67), calls=%async_computation | async-start | bytes 2097152 | tf_op jit(solution)/shard_map/all_to_all | solution.py:47
  36.8 70.5 %all-gather.2.cloned.1.call-start = ((), (), s32[]{:S(2)}) async-start(), calls=%async_computation.4 | async-start | bytes 1769472 | tf_op jit(solution)/shard_map/all_gather | solution.py:22
  66.5 35.9 %all-to-all-start.1 = ((bf16[64,12,448]{2,1,0:T(8,128)(2,1)}), bf16[64,12,448]{2,1,0:T(8,128)(2,1)}, u32[]{:S(2)}, u32[]{:S(2)}) async-start(bf16[64,12,448]{2,1,0:T(8,128)(2,1)} %reshape.69), calls=%async_computation.1 | async-start | bytes 2097152 | tf_op jit(solution)/shard_map/all_to_all | solution.py:47
  73.1 99.3 %reduce-scatter.2.cloned.1.call-start = ((), (), s32[]{:S(2)}) async-start(), calls=%async_computation.3 | async-start | bytes 1769472 | tf_op jit(solution)/shard_map/reduce_scatter | solution.py:72
  74.4 29.6 %copy-start.1 = (bf16[768,448]{1,0:T(8,128)(2,1)S(1)}, bf16[768,448]{1,0:T(8,128)(2,1)}, u32[]{:S(2)}) copy-start(bf16[768,448]{1,0:T(8,128)(2,1)} %reshape.68) | copy-start | bytes 2064388
  107.4 63.0 %copy-start.7 = (bf16[1024,768]{1,0:T(8,128)(2,1)S(1)}, bf16[1024,768]{1,0:T(8,128)(2,1)}, u32[]{:S(2)}) copy-start(bf16[1024,768]{1,0:T(8,128)(2,1)} %all-gather.2.cloned.1.call-done) | copy-start | bytes 4718596
  110.0 62.4 %copy-start.3 = (bf16[1,1,128,768]{3,2,1,0:T(8,128)(2,1)S(1)}, bf16[1,1,128,768]{3,2,1,0:T(8,128)(2,1)}, u32[]{:S(2)}) copy-start(bf16[1,1,128,768]{3,2,1,0:T(8,128)(2,1)} %param.10) | copy-start | bytes 589828
  110.1 62.4 %copy-start.5 = (bf16[1,1,128,768]{3,2,1,0:T(8,128)(2,1)S(1)}, bf16[1,1,128,768]{3,2,1,0:T(8,128)(2,1)}, u32[]{:S(2)}) copy-start(bf16[1,1,128,768]{3,2,1,0:T(8,128)(2,1)} %param.11) | copy-start | bytes 589828
  110.1 60.2 %collective-permute-start = (bf16[448,1024]{1,0:T(8,128)(2,1)S(1)}, bf16[448,1024]{1,0:T(8,128)(2,1)S(1)}, u32[]{:S(2)}, u32[]{:S(2)}) collective-permute-start(bf16[448,1024]{1,0:T(8,128)(2,1)S(1)} %convolution_convert_fusion), channel_id=1, source_target_pairs={{0,1},{1,0},{2,3},{3,2},{4,5},{5,4},{6,7},{7,6},{8,9},{9,8},{10,11... | collective-permute-start | bytes 2752520 | tf_op jit(solution)/shard_map/ppermute | solution.py:57
Sparse Core Ops, SparseCore 0:
  40.9 41.8 all-gather.1
  107.5 56.0 reduce-scatter.1

commit v3 on v2

--- a/solution.py
+++ b/solution.py
@@ -2,6 +2,45 @@
 import jax.numpy as jnp
 from jax import lax
 from jax.sharding import PartitionSpec as P
+
+
+def scatter_sum_et(part):
+    et_count = lax.axis_size("et")
+    et_index = lax.axis_index("et")
+    rows = part.shape[0] // et_count
+    acc = part.reshape(et_count, rows, part.shape[1])
+    step = 1
+    while step < et_count:
+        groups = acc.reshape(acc.shape[0] // 2, 2, rows, part.shape[1])
+        bit = (et_index // step) % 2
+        keep = lax.dynamic_index_in_dim(groups, bit, axis=1, keepdims=False)
+        away = lax.dynamic_index_in_dim(groups, 1 - bit, axis=1, keepdims=False)
+        got = lax.ppermute(
+            away.astype(jnp.bfloat16), "et", [(i, i ^ step) for i in range(et_count)]
+        )
+        acc = keep.astype(jnp.float32) + got.astype(jnp.float32)
+        step *= 2
+    return acc[0]
+
+
+def send_to_partner(block):
+    et_count = lax.axis_size("et")
+    rep_count = lax.axis_size("rep")
+    far = et_count // 2
+
+    def linear(et, rep):
+        return et * rep_count + rep
+
+    across = [
+        (linear(et, rep), linear(et ^ far, rep ^ 1)) for et in range(et_count) for rep in range(rep_count)
+    ]
+    along = [(et, et ^ far) for et in range(et_count)]
+    first, second = jnp.split(block, 2, axis=0)
+    first_hop = lax.ppermute(first, "et", along)
+    second_hop = lax.ppermute(second, ("et", "rep"), across)
+    first_got = lax.ppermute(first_hop, ("et", "rep"), across)
+    second_got = lax.ppermute(second_hop, "et", along)
+    return jnp.concatenate([first_got, second_got], axis=0)
 
 
 def local(grad_out, combine, routing, expert_down_matrix, gate_pre, up_pre):
@@ -54,27 +93,23 @@
     away_part = lax.dot_general(
         away_rows, activation_all, (((0,), (1,)), ((), ())), preferred_element_type=jnp.float32
     ).astype(jnp.bfloat16)
-    received = lax.ppermute(away_part, "rep", [(0, 1), (1, 0)])
+    received = send_to_partner(away_part)
     own_rows = routed(lax.dynamic_slice_in_dim(grad_out, own_at, half, axis=1))
 
     weight_rows = expert_down_matrix[0]
-    block_sum = lax.dot_general(
+    away_sum = lax.dot_general(
         lax.dynamic_slice_in_dim(weight_rows, away_at, half, axis=0),
         away_rows,
         (((0,), (1,)), ((), ())),
         preferred_element_type=jnp.float32,
-    ) + lax.dot_general(
+    )
+    block_sum = away_sum + lax.dot_general(
         lax.dynamic_slice_in_dim(weight_rows, own_at, half, axis=0),
         own_rows,
         (((0,), (1,)), ((), ())),
         preferred_element_type=jnp.float32,
     )
-    act_grad = lax.psum_scatter(
-        block_sum.astype(jnp.bfloat16),
-        "et",
-        scatter_dimension=0,
-        tiled=True,
-    ).astype(jnp.float32)
+    act_grad = scatter_sum_et(block_sum.astype(jnp.bfloat16))
     grad_gate = (
         act_grad * up_vals * gate_sig * (1.0 + gate_activation_values * (1.0 - gate_sig))
     ).astype(jnp.bfloat16)

time: 182 us -> 202 us (1.11)
  the two profiles are of different devices: /device:TPU:56 before, /device:TPU:22 now
where the time goes in v3:
time: 202 us; the launch traced here: 201 us
  waiting for transfers between devices  88.9 us (44%)
  starting transfers between devices  62.4 us (31%)
  local copies, waits for them, and re-layouts  16.2 us (8%)
  between operations  14.5 us (7%)
  matrix products  11.5 us (6%)
  other arithmetic  7.17 us (4%)
    all_to_all x2, waiting for transfers between devices, routed(): sent = lax.all_to_all(rows, 'ep', split_axis=0, concat_axis=0, tiled=True)  49.1 us
    all_to_all x2, starting transfers between devices, routed(): sent = lax.all_to_all(rows, 'ep', split_axis=0, concat_axis=0, tiled=True)  30.1 us
    ppermute x3, waiting for transfers between devices, scatter_sum_et(): lax.ppermute(away.astype(jnp.bfloat16), 'et', [(i, i ^ step) for i in ran...  23 us
    ppermute x1, waiting for transfers between devices, send_to_partner(): first_hop = lax.ppermute(first, 'et', along)  16.7 us
    ppermute x1, starting transfers between devices, send_to_partner(): second_got = lax.ppermute(second_hop, 'et', along)  13.6 us
    ppermute x3, starting transfers between devices, scatter_sum_et(): lax.ppermute(away.astype(jnp.bfloat16), 'et', [(i, i ^ step) for i in ran...  6.22 us
    ppermute x1, starting transfers between devices, send_to_partner(): second_hop = lax.ppermute(second, ('et', 'rep'), across)  5.54 us
    ppermute x1, starting transfers between devices, send_to_partner(): first_got = lax.ppermute(first_hop, ('et', 'rep'), across)  4.31 us
  transfers between devices with their start and end apart: 10, of which 5 were waited for; matrix products, arithmetic and copies ran while one was open for 12% of the time, Pallas kernels for 0%

profile of v3, /device:TPU:22, one launch (start us, length us, event | category | flops | bytes accessed | tf_op | source)
XLA Modules:
  0.0 200.7 jit_solution(16259134994832252621)
XLA Ops:
  7.2 1.0 copy.29
  8.5 1.2 reduce-window.6
  12.7 1.2 reshape.78
  13.9 23.3 %all-to-all-start = ((bf16[64,12,448]{2,1,0:T(8,128)(2,1)}), bf16[64,12,448]{2,1,0:T(8,128)(2,1)S(1)}, u32[]{:S(2)}, u32[]{:S(2)}) async-start(bf16[64,12,448]{2,1,0:T(8,128)(2,1)} %reshape.78), calls=%async_computation | async-start | bytes 2097152 | tf_op jit(solution)/shard_map/all_to_all | solution.py:86
  37.2 2.4 %fusion.2 = bf16[768,448]{0,1:T(8,128)(2,1)} fusion(pred[768,256]{1,0:T(8,128)(4,1)S(1)} %fusion, f32[768]{0:T(1024)S(1)} %select_reduce_fusion, bf16[256,896]{1,0:T(8,128)(2,1)} %param.6, s32[]{:T(128)S(6)} %select_n.58), kind=kOutput, calls=%fused_computation.12 | convolution fusion | flops 176848896 | bytes 1149956 | tf_op jit(solution)/shard_map/dot_general | solution.py:81
  39.6 2.3 %copy.35 = bf16[768,448]{1,0:T(8,128)(2,1)} copy(bf16[768,448]{0,1:T(8,128)(2,1)} %fusion.2) | data formatting | bytes 1376256 | tf_op jit(solution)/shard_map/convert_element_type | solution.py:84
  41.9 2.3 %reshape.80 = bf16[64,12,448]{2,1,0:T(8,128)(2,1)} reshape(bf16[768,448]{1,0:T(8,128)(2,1)} %copy.35) | data formatting | bytes 1376256 | tf_op jit(solution)/shard_map/reshape | solution.py:85
  44.2 22.4 %all-to-all-done = bf16[64,12,448]{2,1,0:T(8,128)(2,1)S(1)} async-done(((bf16[64,12,448]{2,1,0:T(8,128)(2,1)}), bf16[64,12,448]{2,1,0:T(8,128)(2,1)S(1)}, u32[]{:S(2)}, u32[]{:S(2)}) %all-to-all-start) | async-done | bytes 688160 | tf_op jit(solution)/shard_map/all_to_all | solution.py:86
  66.6 6.8 %all-to-all-start.1 = ((bf16[64,12,448]{2,1,0:T(8,128)(2,1)}), bf16[64,12,448]{2,1,0:T(8,128)(2,1)}, u32[]{:S(2)}, u32[]{:S(2)}) async-start(bf16[64,12,448]{2,1,0:T(8,128)(2,1)} %reshape.80), calls=%async_computation.1 | async-start | bytes 2097152 | tf_op jit(solution)/shard_map/all_to_all | solution.py:86
  74.4 1.3 reshape.79
  75.7 26.7 %all-to-all-done.1 = bf16[64,12,448]{2,1,0:T(8,128)(2,1)} async-done(((bf16[64,12,448]{2,1,0:T(8,128)(2,1)}), bf16[64,12,448]{2,1,0:T(8,128)(2,1)}, u32[]{:S(2)}, u32[]{:S(2)}) %all-to-all-start.1) | async-done | bytes 688160 | tf_op jit(solution)/shard_map/all_to_all | solution.py:86
  102.3 2.2 %reshape.81 = bf16[768,448]{1,0:T(8,128)(2,1)} reshape(bf16[64,12,448]{2,1,0:T(8,128)(2,1)} %all-to-all-done.1) | data formatting | bytes 1376256 | tf_op jit(solution)/shard_map/reshape | solution.py:87
  104.6 1.1 fusion.5
  105.7 1.1 add_convert_fusion
  106.8 0.9 dynamic-slice_bitcast_fusion
  107.8 1.9 collective-permute-start
  109.7 2.6 %collective-permute-done = bf16[4,128,768]{2,1,0:T(8,128)(2,1)} collective-permute-done((bf16[4,128,768]{2,1,0:T(8,128)(2,1)}, bf16[4,128,768]{2,1,0:T(8,128)(2,1)}, u32[]{:S(2)}, u32[]{:S(2)}) %collective-permute-start) | collective-permute-done | bytes 786464 | tf_op jit(solution)/shard_map/ppermute | solution.py:18
  112.3 1.3 convert_add_fusion
  113.7 1.1 copy-done.1
  115.6 2.4 %collective-permute-start.1 = (bf16[2,128,768]{2,1,0:T(8,128)(2,1)}, bf16[2,128,768]{2,1,0:T(8,128)(2,1)}, u32[]{:S(2)}, u32[]{:S(2)}) collective-permute-start(bf16[2,128,768]{2,1,0:T(8,128)(2,1)} %fusion.21), channel_id=1, source_target_pairs={{0,4},{2,6},{4,0},{6,2},{8,12},{10,14},{12,8},{14,10},{1,5},{3,7},... | collective-permute-start | bytes 1179656 | tf_op jit(solution)/shard_map/ppermute | solution.py:18
  118.0 2.8 %convolution_convert_fusion = bf16[448,1024]{1,0:T(8,128)(2,1)S(1)} fusion(bf16[768,448]{1,0:T(8,128)(2,1)} %reshape.79, bf16[1024,768]{1,0:T(8,128)(2,1)} %all-gather.2.cloned.1.call-done), kind=kOutput, calls=%fused_computation.7 | convolution fusion | flops 705101824 | bytes 3178496 | tf_op jit(solution)/shard_map/dot_general | solution.py:93
  120.8 1.0 fusion.34
  121.8 2.6 %collective-permute-start.3 = (bf16[224,1024]{1,0:T(8,128)(2,1)}, bf16[224,1024]{1,0:T(8,128)(2,1)}, u32[]{:S(2)}, u32[]{:S(2)}) collective-permute-start(bf16[224,1024]{1,0:T(8,128)(2,1)} %get-tuple-element.11), channel_id=1, source_target_pairs={{0,8},{2,10},{4,12},{6,14},{8,0},{10,2},{12,4},{14,6},{1,9},{3,11}... | collective-permute-start | bytes 1376264 | tf_op jit(solution)/shard_map/ppermute | solution.py:39
  124.4 5.5 %collective-permute-start.5 = (bf16[224,1024]{1,0:T(8,128)(2,1)}, bf16[224,1024]{1,0:T(8,128)(2,1)}, u32[]{:S(2)}, u32[]{:S(2)}) collective-permute-start(bf16[224,1024]{1,0:T(8,128)(2,1)} %get-tuple-element.12), channel_id=1, source_target_pairs={{0,9},{1,8},{2,11},{3,10},{4,13},{5,12},{6,15},{7,14},{8,1},{9,0},... | collective-permute-start | bytes 1376264 | tf_op jit(solution)/shard_map/ppermute | solution.py:40
  130.0 1.1 bitcast_add_fusion
  131.1 16.7 %collective-permute-done.3 = bf16[224,1024]{1,0:T(8,128)(2,1)} collective-permute-done((bf16[224,1024]{1,0:T(8,128)(2,1)}, bf16[224,1024]{1,0:T(8,128)(2,1)}, u32[]{:S(2)}, u32[]{:S(2)}) %collective-permute-start.3) | collective-permute-done | bytes 458784 | tf_op jit(solution)/shard_map/ppermute | solution.py:39
  147.8 4.3 %collective-permute-start.4 = (bf16[224,1024]{1,0:T(8,128)(2,1)}, bf16[224,1024]{1,0:T(8,128)(2,1)S(1)}, u32[]{:S(2)}, u32[]{:S(2)}) collective-permute-start(bf16[224,1024]{1,0:T(8,128)(2,1)} %collective-permute-done.3), channel_id=1, source_target_pairs={{0,9},{1,8},{2,11},{3,10},{4,13},{5,12},{6,15},{7,14},{8,1},{9,0},... | collective-permute-start | bytes 1376264 | tf_op jit(solution)/shard_map/ppermute | solution.py:41
  152.2 13.6 %collective-permute-start.6 = (bf16[224,1024]{1,0:T(8,128)(2,1)}, bf16[224,1024]{1,0:T(8,128)(2,1)}, u32[]{:S(2)}, u32[]{:S(2)}) collective-permute-start(bf16[224,1024]{1,0:T(8,128)(2,1)} %collective-permute-done.5), channel_id=1, source_target_pairs={{0,8},{2,10},{4,12},{6,14},{8,0},{10,2},{12,4},{14,6},{1,9},{3,11}... | collective-permute-start | bytes 1376264 | tf_op jit(solution)/shard_map/ppermute | solution.py:42
  165.8 1.9 collective-permute-start.2
  167.8 20.4 %collective-permute-done.2 = bf16[1,128,768]{2,1,0:T(8,128)(2,1)S(1)} collective-permute-done((bf16[1,128,768]{2,1,0:T(8,128)(2,1)S(1)}, bf16[1,128,768]{2,1,0:T(8,128)(2,1)S(1)}, u32[]{:S(2)}, u32[]{:S(2)}) %collective-permute-start.2) | collective-permute-done | bytes 196640 | tf_op jit(solution)/shard_map/ppermute | solution.py:18
  188.2 2.1 %fusion.20 = (bf16[1,1,128,768]{3,2,1,0:T(8,128)(2,1)}, bf16[1,1,128,768]{3,2,1,0:T(8,128)(2,1)}) fusion(bf16[1,1,128,768]{3,2,1,0:T(8,128)(2,1)} %param.10, bf16[1,128,768]{2,1,0:T(8,128)(2,1)S(1)} %collective-permute-done.2, f32[2,128,768]{2,1,0:T(8,128)} %copy-done.5, s32[]{:T(128)S(6)} %select_n.68, bf16[1,1,128,768]{3,2,1,0:T(8,128)(2,1)} %param.11), kind=kLoop, calls=%fused_computation.38 | loop fusion | flops 1671168 | bytes 1376260 | tf_op jit(solution)/shard_map/convert_element_type | solution.py:116
  190.3 3.6 %fusion.3 = bf16[1,448,1024]{2,1,0:T(8,128)(2,1)} fusion(bf16[224,1024]{1,0:T(8,128)(2,1)} %collective-permute-done.6, bf16[224,1024]{1,0:T(8,128)(2,1)S(1)} %collective-permute-done.4, bf16[768,448]{1,0:T(8,128)(2,1)S(1)} %copy-done.4, bf16[1024,768]{1,0:T(8,128)(2,1)} %all-gather.2.cloned.1.call-done), kind=kOutput, calls=%fused_computation.13 | convolution fusion | flops 708313088 | bytes 4096000 | tf_op jit(solution)/shard_map/dot_general | solution.py:118
  (48 shorter events, 5.1 us)
Async XLA Ops:
  7.2 97.4 %copy-start = (bf16[1,896,1024]{2,1,0:T(8,128)(2,1)S(1)}, bf16[1,896,1024]{2,1,0:T(8,128)(2,1)}, u32[]{:S(2)}) copy-start(bf16[1,896,1024]{2,1,0:T(8,128)(2,1)} %param.9) | copy-start | bytes 5505028
  7.2 4.1 %copy-start.9 = (s32[256,2]{0,1:T(2,128)S(1)}, s32[256,2]{0,1:T(2,128)}, u32[]{:S(2)}) copy-start(s32[256,2]{0,1:T(2,128)} %param.8) | copy-start | bytes 6148
  7.2 4.6 %copy-start.10 = (bf16[256,896]{1,0:T(8,128)(2,1)S(1)}, bf16[256,896]{1,0:T(8,128)(2,1)}, u32[]{:S(2)}) copy-start(bf16[256,896]{1,0:T(8,128)(2,1)} %param.6) | copy-start | bytes 1376260
  13.9 52.7 %all-to-all-start = ((bf16[64,12,448]{2,1,0:T(8,128)(2,1)}), bf16[64,12,448]{2,1,0:T(8,128)(2,1)S(1)}, u32[]{:S(2)}, u32[]{:S(2)}) async-start(bf16[64,12,448]{2,1,0:T(8,128)(2,1)} %reshape.78), calls=%async_computation | async-start | bytes 2097152 | tf_op jit(solution)/shard_map/all_to_all | solution.py:86
  41.9 31.6 %copy-start.7 = (bf16[1,1,128,768]{3,2,1,0:T(8,128)(2,1)S(1)}, bf16[1,1,128,768]{3,2,1,0:T(8,128)(2,1)}, u32[]{:S(2)}) copy-start(bf16[1,1,128,768]{3,2,1,0:T(8,128)(2,1)} %param.10) | copy-start | bytes 589828
  41.9 31.6 %copy-start.8 = (bf16[1,1,128,768]{3,2,1,0:T(8,128)(2,1)S(1)}, bf16[1,1,128,768]{3,2,1,0:T(8,128)(2,1)}, u32[]{:S(2)}) copy-start(bf16[1,1,128,768]{3,2,1,0:T(8,128)(2,1)} %param.11) | copy-start | bytes 589828
  66.6 35.7 %all-to-all-start.1 = ((bf16[64,12,448]{2,1,0:T(8,128)(2,1)}), bf16[64,12,448]{2,1,0:T(8,128)(2,1)}, u32[]{:S(2)}, u32[]{:S(2)}) async-start(bf16[64,12,448]{2,1,0:T(8,128)(2,1)} %reshape.80), calls=%async_computation.1 | async-start | bytes 2097152 | tf_op jit(solution)/shard_map/all_to_all | solution.py:86
  73.5 44.6 %all-gather.2.cloned.1.call-start = ((), (), s32[]{:S(2)}) async-start(), calls=%async_computation.2 | async-start | bytes 1769472 | tf_op jit(solution)/shard_map/all_gather | solution.py:61
  75.6 28.9 %copy-start.6 = (bf16[768,448]{1,0:T(8,128)(2,1)S(1)}, bf16[768,448]{1,0:T(8,128)(2,1)}, u32[]{:S(2)}) copy-start(bf16[768,448]{1,0:T(8,128)(2,1)} %reshape.79) | copy-start | bytes 2064388
  104.6 1.2 copy-start.3
  107.8 4.6 %collective-permute-start = (bf16[4,128,768]{2,1,0:T(8,128)(2,1)}, bf16[4,128,768]{2,1,0:T(8,128)(2,1)}, u32[]{:S(2)}, u32[]{:S(2)}) collective-permute-start(bf16[4,128,768]{2,1,0:T(8,128)(2,1)} %dynamic-slice_bitcast_fusion), channel_id=1, source_target_pairs={{0,2},{2,0},{4,6},{6,4},{8,10},{10,8},{12,14},{14,12},{1,3},{3,1},... | collective-permute-start | bytes 2359304 | tf_op jit(solution)/shard_map/ppermute | solution.py:18
  113.6 1.1 copy-start.1
  115.6 14.4 %collective-permute-start.1 = (bf16[2,128,768]{2,1,0:T(8,128)(2,1)}, bf16[2,128,768]{2,1,0:T(8,128)(2,1)}, u32[]{:S(2)}, u32[]{:S(2)}) collective-permute-start(bf16[2,128,768]{2,1,0:T(8,128)(2,1)} %fusion.21), channel_id=1, source_target_pairs={{0,4},{2,6},{4,0},{6,2},{8,12},{10,14},{12,8},{14,10},{1,5},{3,7},... | collective-permute-start | bytes 1179656 | tf_op jit(solution)/shard_map/ppermute | solution.py:18
  120.8 9.2 %copy-start.2 = (f32[4,128,768]{2,1,0:T(8,128)S(1)}, f32[4,128,768]{2,1,0:T(8,128)}, u32[]{:S(2)}) copy-start(f32[4,128,768]{2,1,0:T(8,128)} %copy-done.1) | copy-start | bytes 4718596
  121.8 26.0 %collective-permute-start.3 = (bf16[224,1024]{1,0:T(8,128)(2,1)}, bf16[224,1024]{1,0:T(8,128)(2,1)}, u32[]{:S(2)}, u32[]{:S(2)}) collective-permute-start(bf16[224,1024]{1,0:T(8,128)(2,1)} %get-tuple-element.11), channel_id=1, source_target_pairs={{0,8},{2,10},{4,12},{6,14},{8,0},{10,2},{12,4},{14,6},{1,9},{3,11}... | collective-permute-start | bytes 1376264 | tf_op jit(solution)/shard_map/ppermute | solution.py:39
  124.4 27.7 %collective-permute-start.5 = (bf16[224,1024]{1,0:T(8,128)(2,1)}, bf16[224,1024]{1,0:T(8,128)(2,1)}, u32[]{:S(2)}, u32[]{:S(2)}) collective-permute-start(bf16[224,1024]{1,0:T(8,128)(2,1)} %get-tuple-element.12), channel_id=1, source_target_pairs={{0,9},{1,8},{2,11},{3,10},{4,13},{5,12},{6,15},{7,14},{8,1},{9,0},... | collective-permute-start | bytes 1376264 | tf_op jit(solution)/shard_map/ppermute | solution.py:40
  131.1 34.7 %copy-start.5 = (f32[2,128,768]{2,1,0:T(8,128)}, f32[2,128,768]{2,1,0:T(8,128)S(1)}, u32[]{:S(2)}) copy-start(f32[2,128,768]{2,1,0:T(8,128)S(1)} %bitcast_add_fusion) | copy-start | bytes 2359300
  131.1 59.2 %copy-start.4 = (bf16[768,448]{1,0:T(8,128)(2,1)S(1)}, bf16[768,448]{1,0:T(8,128)(2,1)}, u32[]{:S(2)}) copy-start(bf16[768,448]{1,0:T(8,128)(2,1)} %reshape.81) | copy-start | bytes 2064388
  147.8 42.5 %collective-permute-start.4 = (bf16[224,1024]{1,0:T(8,128)(2,1)}, bf16[224,1024]{1,0:T(8,128)(2,1)S(1)}, u32[]{:S(2)}, u32[]{:S(2)}) collective-permute-start(bf16[224,1024]{1,0:T(8,128)(2,1)} %collective-permute-done.3), channel_id=1, source_target_pairs={{0,9},{1,8},{2,11},{3,10},{4,13},{5,12},{6,15},{7,14},{8,1},{9,0},... | collective-permute-start | bytes 1376264 | tf_op jit(solution)/shard_map/ppermute | solution.py:41
  152.2 38.1 %collective-permute-start.6 = (bf16[224,1024]{1,0:T(8,128)(2,1)}, bf16[224,1024]{1,0:T(8,128)(2,1)}, u32[]{:S(2)}, u32[]{:S(2)}) collective-permute-start(bf16[224,1024]{1,0:T(8,128)(2,1)} %collective-permute-done.5), channel_id=1, source_target_pairs={{0,8},{2,10},{4,12},{6,14},{8,0},{10,2},{12,4},{14,6},{1,9},{3,11}... | collective-permute-start | bytes 1376264 | tf_op jit(solution)/shard_map/ppermute | solution.py:42
  165.8 22.4 %collective-permute-start.2 = (bf16[1,128,768]{2,1,0:T(8,128)(2,1)S(1)}, bf16[1,128,768]{2,1,0:T(8,128)(2,1)S(1)}, u32[]{:S(2)}, u32[]{:S(2)}) collective-permute-start(bf16[1,128,768]{2,1,0:T(8,128)(2,1)S(1)} %dynamic-slice_convert_fusion.1), channel_id=1, source_target_pairs={{0,8},{2,10},{4,12},{6,14},{8,0},{10,2},{12,4},{14,6},{1,9},{3,11}... | collective-permute-start | bytes 589832 | tf_op jit(solution)/shard_map/ppermute | solution.py:18
Sparse Core Ops, SparseCore 0:
  77.5 40.3 all-gather.1

commit v4 on v3

--- a/solution.py
+++ b/solution.py
@@ -21,26 +21,6 @@
         acc = keep.astype(jnp.float32) + got.astype(jnp.float32)
         step *= 2
     return acc[0]
-
-
-def send_to_partner(block):
-    et_count = lax.axis_size("et")
-    rep_count = lax.axis_size("rep")
-    far = et_count // 2
-
-    def linear(et, rep):
-        return et * rep_count + rep
-
-    across = [
-        (linear(et, rep), linear(et ^ far, rep ^ 1)) for et in range(et_count) for rep in range(rep_count)
-    ]
-    along = [(et, et ^ far) for et in range(et_count)]
-    first, second = jnp.split(block, 2, axis=0)
-    first_hop = lax.ppermute(first, "et", along)
-    second_hop = lax.ppermute(second, ("et", "rep"), across)
-    first_got = lax.ppermute(first_hop, ("et", "rep"), across)
-    second_got = lax.ppermute(second_hop, "et", along)
-    return jnp.concatenate([first_got, second_got], axis=0)
 
 
 def local(grad_out, combine, routing, expert_down_matrix, gate_pre, up_pre):
@@ -93,17 +73,22 @@
     away_part = lax.dot_general(
         away_rows, activation_all, (((0,), (1,)), ((), ())), preferred_element_type=jnp.float32
     ).astype(jnp.bfloat16)
-    received = send_to_partner(away_part)
+    first, second = jnp.split(away_part, 2, axis=0)
+    first_got = lax.ppermute(first, "rep", [(0, 1), (1, 0)])
+    swapped = lax.all_to_all(
+        jnp.broadcast_to(second[None], (rep_count,) + second.shape), "rep", 0, 0, tiled=True
+    )
+    second_got = lax.dynamic_index_in_dim(swapped, 1 - rep_index, axis=0, keepdims=False)
+    received = jnp.concatenate([first_got, second_got], axis=0)
     own_rows = routed(lax.dynamic_slice_in_dim(grad_out, own_at, half, axis=1))
 
     weight_rows = expert_down_matrix[0]
-    away_sum = lax.dot_general(
+    block_sum = lax.dot_general(
         lax.dynamic_slice_in_dim(weight_rows, away_at, half, axis=0),
         away_rows,
         (((0,), (1,)), ((), ())),
         preferred_element_type=jnp.float32,
-    )
-    block_sum = away_sum + lax.dot_general(
+    ) + lax.dot_general(
         lax.dynamic_slice_in_dim(weight_rows, own_at, half, axis=0),
         own_rows,
         (((0,), (1,)), ((), ())),

time: 202 us -> 197 us (0.975)
  the two profiles are of different devices: /device:TPU:22 before, /device:TPU:1 now
where the time goes in v4:
time: 197 us; the launch traced here: 196 us
  waiting for transfers between devices  87 us (44%)
  starting transfers between devices  56.5 us (29%)
  local copies, waits for them, and re-layouts  19 us (10%)
  between operations  14.4 us (7%)
  matrix products  11.5 us (6%)
  other arithmetic  7.17 us (4%)
    all_to_all x2, waiting for transfers between devices, routed(): sent = lax.all_to_all(rows, 'ep', split_axis=0, concat_axis=0, tiled=True)  44.1 us
    ppermute x3, waiting for transfers between devices, scatter_sum_et(): lax.ppermute(away.astype(jnp.bfloat16), 'et', [(i, i ^ step) for i in ran...  41.5 us
    all_to_all x2, starting transfers between devices, routed(): sent = lax.all_to_all(rows, 'ep', split_axis=0, concat_axis=0, tiled=True)  33.1 us
    ppermute x3, starting transfers between devices, scatter_sum_et(): lax.ppermute(away.astype(jnp.bfloat16), 'et', [(i, i ^ step) for i in ran...  12.2 us
    ppermute x1, starting transfers between devices, local(): first_got = lax.ppermute(first, 'rep', [(0, 1), (1, 0)])  6.91 us
    all_to_all x1, starting transfers between devices, local(): lax.all_to_all(jnp.broadcast_to(second[None], (rep_count,) + second.shape...  4.35 us
  transfers between devices with their start and end apart: 8, of which 5 were waited for; matrix products, arithmetic and copies ran while one was open for 13% of the time, Pallas kernels for 0%

profile of v4, /device:TPU:1, one launch (start us, length us, event | category | flops | bytes accessed | tf_op | source)
XLA Modules:
  0.0 195.6 jit_solution(2128814167708025702)
XLA Ops:
  7.2 1.0 copy.29
  8.5 1.2 reduce-window.6
  12.7 1.2 reshape.79
  13.9 23.9 %all-to-all-start = ((bf16[64,12,448]{2,1,0:T(8,128)(2,1)}), bf16[64,12,448]{2,1,0:T(8,128)(2,1)S(1)}, u32[]{:S(2)}, u32[]{:S(2)}) async-start(bf16[64,12,448]{2,1,0:T(8,128)(2,1)} %reshape.79), calls=%async_computation | async-start | bytes 2097152 | tf_op jit(solution)/shard_map/all_to_all | solution.py:66
  37.9 2.4 %fusion.2 = bf16[768,448]{0,1:T(8,128)(2,1)} fusion(pred[768,256]{1,0:T(8,128)(4,1)S(1)} %fusion, f32[768]{0:T(1024)S(1)} %select_reduce_fusion, bf16[256,896]{1,0:T(8,128)(2,1)} %param.6, s32[]{:T(128)S(6)} %select_n.62), kind=kOutput, calls=%fused_computation.12 | convolution fusion | flops 176848896 | bytes 1149956 | tf_op jit(solution)/shard_map/dot_general | solution.py:61
  40.3 2.3 %copy.35 = bf16[768,448]{1,0:T(8,128)(2,1)} copy(bf16[768,448]{0,1:T(8,128)(2,1)} %fusion.2) | data formatting | bytes 1376256 | tf_op jit(solution)/shard_map/convert_element_type | solution.py:64
  42.6 2.3 %reshape.81 = bf16[64,12,448]{2,1,0:T(8,128)(2,1)} reshape(bf16[768,448]{1,0:T(8,128)(2,1)} %copy.35) | data formatting | bytes 1376256 | tf_op jit(solution)/shard_map/reshape | solution.py:65
  44.9 19.8 %all-to-all-done = bf16[64,12,448]{2,1,0:T(8,128)(2,1)S(1)} async-done(((bf16[64,12,448]{2,1,0:T(8,128)(2,1)}), bf16[64,12,448]{2,1,0:T(8,128)(2,1)S(1)}, u32[]{:S(2)}, u32[]{:S(2)}) %all-to-all-start) | async-done | bytes 688160 | tf_op jit(solution)/shard_map/all_to_all | solution.py:66
  64.7 9.1 %all-to-all-start.1 = ((bf16[64,12,448]{2,1,0:T(8,128)(2,1)}), bf16[64,12,448]{2,1,0:T(8,128)(2,1)}, u32[]{:S(2)}, u32[]{:S(2)}) async-start(bf16[64,12,448]{2,1,0:T(8,128)(2,1)} %reshape.81), calls=%async_computation.1 | async-start | bytes 2097152 | tf_op jit(solution)/shard_map/all_to_all | solution.py:66
  74.7 1.3 reshape.80
  76.0 24.3 %all-to-all-done.1 = bf16[64,12,448]{2,1,0:T(8,128)(2,1)} async-done(((bf16[64,12,448]{2,1,0:T(8,128)(2,1)}), bf16[64,12,448]{2,1,0:T(8,128)(2,1)}, u32[]{:S(2)}, u32[]{:S(2)}) %all-to-all-start.1) | async-done | bytes 688160 | tf_op jit(solution)/shard_map/all_to_all | solution.py:66
  100.3 2.2 %reshape.82 = bf16[768,448]{1,0:T(8,128)(2,1)} reshape(bf16[64,12,448]{2,1,0:T(8,128)(2,1)} %all-to-all-done.1) | data formatting | bytes 1376256 | tf_op jit(solution)/shard_map/reshape | solution.py:67
  102.5 1.1 fusion.5
  103.7 1.1 add_convert_fusion
  104.8 0.9 dynamic-slice_bitcast_fusion
  105.7 6.0 %collective-permute-start = (bf16[4,128,768]{2,1,0:T(8,128)(2,1)}, bf16[4,128,768]{2,1,0:T(8,128)(2,1)}, u32[]{:S(2)}, u32[]{:S(2)}) collective-permute-start(bf16[4,128,768]{2,1,0:T(8,128)(2,1)} %dynamic-slice_bitcast_fusion), channel_id=1, source_target_pairs={{0,2},{2,0},{4,6},{6,4},{8,10},{10,8},{12,14},{14,12},{1,3},{3,1},... | collective-permute-start | bytes 2359304 | tf_op jit(solution)/shard_map/ppermute | solution.py:18
  111.7 2.2 %collective-permute-done = bf16[4,128,768]{2,1,0:T(8,128)(2,1)} collective-permute-done((bf16[4,128,768]{2,1,0:T(8,128)(2,1)}, bf16[4,128,768]{2,1,0:T(8,128)(2,1)}, u32[]{:S(2)}, u32[]{:S(2)}) %collective-permute-start) | collective-permute-done | bytes 786464 | tf_op jit(solution)/shard_map/ppermute | solution.py:18
  113.9 1.3 convert_add_fusion
  115.2 1.1 copy-done.1
  117.2 3.1 %collective-permute-start.1 = (bf16[2,128,768]{2,1,0:T(8,128)(2,1)}, bf16[2,128,768]{2,1,0:T(8,128)(2,1)}, u32[]{:S(2)}, u32[]{:S(2)}) collective-permute-start(bf16[2,128,768]{2,1,0:T(8,128)(2,1)} %fusion.21), channel_id=1, source_target_pairs={{0,4},{2,6},{4,0},{6,2},{8,12},{10,14},{12,8},{14,10},{1,5},{3,7},... | collective-permute-start | bytes 1179656 | tf_op jit(solution)/shard_map/ppermute | solution.py:18
  120.3 1.5 all-gather.2.cloned.1.call-done
  121.8 2.8 %convolution_convert_fusion = bf16[448,1024]{1,0:T(8,128)(2,1)S(1)} fusion(bf16[768,448]{1,0:T(8,128)(2,1)} %reshape.80, bf16[1024,768]{1,0:T(8,128)(2,1)} %all-gather.2.cloned.1.call-done), kind=kOutput, calls=%fused_computation.7 | convolution fusion | flops 705101824 | bytes 3178496 | tf_op jit(solution)/shard_map/dot_general | solution.py:73
  125.4 1.0 broadcast_in_dim.33
  126.5 4.4 %all-to-all-start.2 = ((bf16[2,224,1024]{2,1,0:T(8,128)(2,1)}), bf16[2,224,1024]{2,1,0:T(8,128)(2,1)}, u32[]{:S(2)}, u32[]{:S(2)}) async-start(bf16[2,224,1024]{2,1,0:T(8,128)(2,1)} %broadcast_in_dim.33), calls=%async_computation.2 | async-start | bytes 1835008 | tf_op jit(solution)/shard_map/all_to_all | solution.py:78
  130.9 1.1 bitcast_add_fusion
  132.0 0.9 copy-done.5
  132.9 3.1 %collective-permute-start.2 = (bf16[1,128,768]{2,1,0:T(8,128)(2,1)S(1)}, bf16[1,128,768]{2,1,0:T(8,128)(2,1)S(1)}, u32[]{:S(2)}, u32[]{:S(2)}) collective-permute-start(bf16[1,128,768]{2,1,0:T(8,128)(2,1)S(1)} %dynamic-slice_convert_fusion.1), channel_id=1, source_target_pairs={{0,8},{2,10},{4,12},{6,14},{8,0},{10,2},{12,4},{14,6},{1,9},{3,11}... | collective-permute-start | bytes 589832 | tf_op jit(solution)/shard_map/ppermute | solution.py:18
  136.0 6.9 %collective-permute-start.3 = (bf16[224,1024]{1,0:T(8,128)(2,1)}, bf16[224,1024]{1,0:T(8,128)(2,1)S(1)}, u32[]{:S(2)}, u32[]{:S(2)}) collective-permute-start(bf16[224,1024]{1,0:T(8,128)(2,1)} %get-tuple-element.11), channel_id=1, source_target_pairs={{0,1},{1,0},{2,3},{3,2},{4,5},{5,4},{6,7},{7,6},{8,9},{9,8},{10,11... | collective-permute-start | bytes 1376264 | tf_op jit(solution)/shard_map/ppermute | solution.py:77
  142.9 39.3 %collective-permute-done.2 = bf16[1,128,768]{2,1,0:T(8,128)(2,1)S(1)} collective-permute-done((bf16[1,128,768]{2,1,0:T(8,128)(2,1)S(1)}, bf16[1,128,768]{2,1,0:T(8,128)(2,1)S(1)}, u32[]{:S(2)}, u32[]{:S(2)}) %collective-permute-start.2) | collective-permute-done | bytes 196640 | tf_op jit(solution)/shard_map/ppermute | solution.py:18
  182.1 2.1 %fusion.20 = (bf16[1,1,128,768]{3,2,1,0:T(8,128)(2,1)}, bf16[1,1,128,768]{3,2,1,0:T(8,128)(2,1)}) fusion(bf16[1,1,128,768]{3,2,1,0:T(8,128)(2,1)} %param.10, bf16[1,128,768]{2,1,0:T(8,128)(2,1)S(1)} %collective-permute-done.2, f32[2,128,768]{2,1,0:T(8,128)} %copy-done.5, s32[]{:T(128)S(6)} %select_n.72, bf16[1,1,128,768]{3,2,1,0:T(8,128)(2,1)} %param.11), kind=kLoop, calls=%fused_computation.39 | loop fusion | flops 1671168 | bytes 1376260 | tf_op jit(solution)/shard_map/convert_element_type | solution.py:101
  184.2 1.0 dynamic-slice_bitcast_fusion.1
  185.3 3.5 %fusion.3 = bf16[1,448,1024]{2,1,0:T(8,128)(2,1)} fusion(bf16[224,1024]{1,0:T(8,128)(2,1)S(1)} %dynamic-slice_bitcast_fusion.1, bf16[224,1024]{1,0:T(8,128)(2,1)S(1)} %collective-permute-done.3, bf16[768,448]{1,0:T(8,128)(2,1)S(1)} %copy-done.4, bf16[1024,768]{1,0:T(8,128)(2,1)} %all-gather.2.cloned.1.call-done), kind=kOutput, calls=%fused_computation.13 | convolution fusion | flops 708313088 | bytes 4096000 | tf_op jit(solution)/shard_map/dot_general | solution.py:103
  (46 shorter events, 5.9 us)
Async XLA Ops:
  7.2 95.4 %copy-start = (bf16[1,896,1024]{2,1,0:T(8,128)(2,1)S(1)}, bf16[1,896,1024]{2,1,0:T(8,128)(2,1)}, u32[]{:S(2)}) copy-start(bf16[1,896,1024]{2,1,0:T(8,128)(2,1)} %param.9) | copy-start | bytes 5505028
  7.2 4.1 %copy-start.9 = (s32[256,2]{0,1:T(2,128)S(1)}, s32[256,2]{0,1:T(2,128)}, u32[]{:S(2)}) copy-start(s32[256,2]{0,1:T(2,128)} %param.8) | copy-start | bytes 6148
  7.2 4.6 %copy-start.10 = (bf16[256,896]{1,0:T(8,128)(2,1)S(1)}, bf16[256,896]{1,0:T(8,128)(2,1)}, u32[]{:S(2)}) copy-start(bf16[256,896]{1,0:T(8,128)(2,1)} %param.6) | copy-start | bytes 1376260
  13.9 50.8 %all-to-all-start = ((bf16[64,12,448]{2,1,0:T(8,128)(2,1)}), bf16[64,12,448]{2,1,0:T(8,128)(2,1)S(1)}, u32[]{:S(2)}, u32[]{:S(2)}) async-start(bf16[64,12,448]{2,1,0:T(8,128)(2,1)} %reshape.79), calls=%async_computation | async-start | bytes 2097152 | tf_op jit(solution)/shard_map/all_to_all | solution.py:66
  42.6 31.3 %copy-start.7 = (bf16[1,1,128,768]{3,2,1,0:T(8,128)(2,1)S(1)}, bf16[1,1,128,768]{3,2,1,0:T(8,128)(2,1)}, u32[]{:S(2)}) copy-start(bf16[1,1,128,768]{3,2,1,0:T(8,128)(2,1)} %param.10) | copy-start | bytes 589828
  42.6 31.3 %copy-start.8 = (bf16[1,1,128,768]{3,2,1,0:T(8,128)(2,1)S(1)}, bf16[1,1,128,768]{3,2,1,0:T(8,128)(2,1)}, u32[]{:S(2)}) copy-start(bf16[1,1,128,768]{3,2,1,0:T(8,128)(2,1)} %param.11) | copy-start | bytes 589828
  64.7 35.6 %all-to-all-start.1 = ((bf16[64,12,448]{2,1,0:T(8,128)(2,1)}), bf16[64,12,448]{2,1,0:T(8,128)(2,1)}, u32[]{:S(2)}, u32[]{:S(2)}) async-start(bf16[64,12,448]{2,1,0:T(8,128)(2,1)} %reshape.81), calls=%async_computation.1 | async-start | bytes 2097152 | tf_op jit(solution)/shard_map/all_to_all | solution.py:66
  73.8 48.0 %all-gather.2.cloned.1.call-start = ((), (), s32[]{:S(2)}) async-start(), calls=%async_computation.3 | async-start | bytes 1769472 | tf_op jit(solution)/shard_map/all_gather | solution.py:41
  76.0 26.5 %copy-start.6 = (bf16[768,448]{1,0:T(8,128)(2,1)S(1)}, bf16[768,448]{1,0:T(8,128)(2,1)}, u32[]{:S(2)}) copy-start(bf16[768,448]{1,0:T(8,128)(2,1)} %reshape.80) | copy-start | bytes 2064388
  102.5 1.1 copy-start.3
  105.7 8.2 %collective-permute-start = (bf16[4,128,768]{2,1,0:T(8,128)(2,1)}, bf16[4,128,768]{2,1,0:T(8,128)(2,1)}, u32[]{:S(2)}, u32[]{:S(2)}) collective-permute-start(bf16[4,128,768]{2,1,0:T(8,128)(2,1)} %dynamic-slice_bitcast_fusion), channel_id=1, source_target_pairs={{0,2},{2,0},{4,6},{6,4},{8,10},{10,8},{12,14},{14,12},{1,3},{3,1},... | collective-permute-start | bytes 2359304 | tf_op jit(solution)/shard_map/ppermute | solution.py:18
  115.2 1.2 copy-start.1
  117.2 13.7 %collective-permute-start.1 = (bf16[2,128,768]{2,1,0:T(8,128)(2,1)}, bf16[2,128,768]{2,1,0:T(8,128)(2,1)}, u32[]{:S(2)}, u32[]{:S(2)}) collective-permute-start(bf16[2,128,768]{2,1,0:T(8,128)(2,1)} %fusion.21), channel_id=1, source_target_pairs={{0,4},{2,6},{4,0},{6,2},{8,12},{10,14},{12,8},{14,10},{1,5},{3,7},... | collective-permute-start | bytes 1179656 | tf_op jit(solution)/shard_map/ppermute | solution.py:18
  125.4 5.5 %copy-start.2 = (f32[4,128,768]{2,1,0:T(8,128)S(1)}, f32[4,128,768]{2,1,0:T(8,128)}, u32[]{:S(2)}) copy-start(f32[4,128,768]{2,1,0:T(8,128)} %copy-done.1) | copy-start | bytes 4718596
  126.5 57.8 %all-to-all-start.2 = ((bf16[2,224,1024]{2,1,0:T(8,128)(2,1)}), bf16[2,224,1024]{2,1,0:T(8,128)(2,1)}, u32[]{:S(2)}, u32[]{:S(2)}) async-start(bf16[2,224,1024]{2,1,0:T(8,128)(2,1)} %broadcast_in_dim.33), calls=%async_computation.2 | async-start | bytes 1835008 | tf_op jit(solution)/shard_map/all_to_all | solution.py:78
  132.0 0.9 copy-start.5
  132.8 52.5 %copy-start.4 = (bf16[768,448]{1,0:T(8,128)(2,1)S(1)}, bf16[768,448]{1,0:T(8,128)(2,1)}, u32[]{:S(2)}) copy-start(bf16[768,448]{1,0:T(8,128)(2,1)} %reshape.82) | copy-start | bytes 2064388
  132.9 49.3 %collective-permute-start.2 = (bf16[1,128,768]{2,1,0:T(8,128)(2,1)S(1)}, bf16[1,128,768]{2,1,0:T(8,128)(2,1)S(1)}, u32[]{:S(2)}, u32[]{:S(2)}) collective-permute-start(bf16[1,128,768]{2,1,0:T(8,128)(2,1)S(1)} %dynamic-slice_convert_fusion.1), channel_id=1, source_target_pairs={{0,8},{2,10},{4,12},{6,14},{8,0},{10,2},{12,4},{14,6},{1,9},{3,11}... | collective-permute-start | bytes 589832 | tf_op jit(solution)/shard_map/ppermute | solution.py:18
  136.0 49.4 %collective-permute-start.3 = (bf16[224,1024]{1,0:T(8,128)(2,1)}, bf16[224,1024]{1,0:T(8,128)(2,1)S(1)}, u32[]{:S(2)}, u32[]{:S(2)}) collective-permute-start(bf16[224,1024]{1,0:T(8,128)(2,1)} %get-tuple-element.11), channel_id=1, source_target_pairs={{0,1},{1,0},{2,3},{3,2},{4,5},{5,4},{6,7},{7,6},{8,9},{9,8},{10,11... | collective-permute-start | bytes 1376264 | tf_op jit(solution)/shard_map/ppermute | solution.py:77
Sparse Core Ops, SparseCore 0:
  77.9 43.8 all-gather.1

commit v5 on v4

--- a/solution.py
+++ b/solution.py
@@ -18,8 +18,9 @@
         got = lax.ppermute(
             away.astype(jnp.bfloat16), "et", [(i, i ^ step) for i in range(et_count)]
         )
-        acc = keep.astype(jnp.float32) + got.astype(jnp.float32)
+        total = keep.astype(jnp.float32) + got.astype(jnp.float32)
         step *= 2
+        acc = total if step >= et_count else total.astype(jnp.bfloat16)
     return acc[0]
 
 
@@ -73,13 +74,7 @@
     away_part = lax.dot_general(
         away_rows, activation_all, (((0,), (1,)), ((), ())), preferred_element_type=jnp.float32
     ).astype(jnp.bfloat16)
-    first, second = jnp.split(away_part, 2, axis=0)
-    first_got = lax.ppermute(first, "rep", [(0, 1), (1, 0)])
-    swapped = lax.all_to_all(
-        jnp.broadcast_to(second[None], (rep_count,) + second.shape), "rep", 0, 0, tiled=True
-    )
-    second_got = lax.dynamic_index_in_dim(swapped, 1 - rep_index, axis=0, keepdims=False)
-    received = jnp.concatenate([first_got, second_got], axis=0)
+    received = lax.ppermute(away_part, "rep", [(0, 1), (1, 0)])
     own_rows = routed(lax.dynamic_slice_in_dim(grad_out, own_at, half, axis=1))
 
     weight_rows = expert_down_matrix[0]

time: 197 us -> 195 us (0.990)
  waiting for transfers between devices: 87 us -> 94 us
  starting transfers between devices: 56.5 us -> 50.5 us
  local copies, waits for them, and re-layouts: 19 us -> 15.7 us
    ppermute x3, waiting for transfers between devices: 41.5 us -> 48.4 us  [scatter_sum_et(): lax.ppermute(away.astype(jnp.bfloat16), 'et', [(i, i ^ step) for i in ran...]
    all_to_all x1 -> x0, starting transfers between devices: 4.35 us -> none  [local(): lax.all_to_all(jnp.broadcast_to(second[None], (rep_count,) + second.shape...]
    convert_element_type x0 -> x2, other arithmetic: none -> 2.41 us  [scatter_sum_et(): acc = total if step >= et_count else total.astype(jnp.bfloat16)]
    add x2 -> x0, other arithmetic: 2.36 us -> none  [scatter_sum_et(): acc = keep.astype(jnp.float32) + got.astype(jnp.float32)]
    ppermute x1, starting transfers between devices: 6.91 us -> 4.82 us  [local(): received = lax.ppermute(away_part, 'rep', [(0, 1), (1, 0)])]
  transfers between devices with their start and end apart: 8 -> 7, of which waited for: 5 -> 5; matrix products, arithmetic and copies ran while one was open for 13% -> 12% of each run, Pallas kernels for 0% -> 0%
where the time goes in v5:
time: 195 us; the launch traced here: 194 us
  waiting for transfers between devices  94 us (48%)
  starting transfers between devices  50.5 us (26%)
  local copies, waits for them, and re-layouts  15.7 us (8%)
  between operations  14.4 us (7%)
  matrix products  12.7 us (7%)
  other arithmetic  7.21 us (4%)
    ppermute x3, waiting for transfers between devices, scatter_sum_et(): lax.ppermute(away.astype(jnp.bfloat16), 'et', [(i, i ^ step) for i in ran...  48.4 us
    all_to_all x2, waiting for transfers between devices, routed(): sent = lax.all_to_all(rows, 'ep', split_axis=0, concat_axis=0, tiled=True)  44.1 us
    all_to_all x2, starting transfers between devices, routed(): sent = lax.all_to_all(rows, 'ep', split_axis=0, concat_axis=0, tiled=True)  33.1 us
    ppermute x3, starting transfers between devices, scatter_sum_et(): lax.ppermute(away.astype(jnp.bfloat16), 'et', [(i, i ^ step) for i in ran...  12.6 us
    ppermute x1, starting transfers between devices, local(): received = lax.ppermute(away_part, 'rep', [(0, 1), (1, 0)])  4.82 us
  transfers between devices with their start and end apart: 7, of which 5 were waited for; matrix products, arithmetic and copies ran while one was open for 12% of the time, Pallas kernels for 0%

profile of v5, /device:TPU:1, one launch (start us, length us, event | category | flops | bytes accessed | tf_op | source)
XLA Modules:
  0.0 194.5 jit_solution(627756013298533427)
XLA Ops:
  7.2 1.0 copy.29
  8.5 1.2 reduce-window.6
  10.3 0.8 copy.33
  12.7 1.2 reshape.79
  13.9 23.9 %all-to-all-start = ((bf16[64,12,448]{2,1,0:T(8,128)(2,1)}), bf16[64,12,448]{2,1,0:T(8,128)(2,1)S(1)}, u32[]{:S(2)}, u32[]{:S(2)}) async-start(bf16[64,12,448]{2,1,0:T(8,128)(2,1)} %reshape.79), calls=%async_computation | async-start | bytes 2097152 | tf_op jit(solution)/shard_map/all_to_all | solution.py:67
  37.9 2.4 %fusion.3 = bf16[768,448]{0,1:T(8,128)(2,1)} fusion(pred[768,256]{1,0:T(8,128)(4,1)S(1)} %fusion.1, f32[768]{0:T(1024)S(1)} %select_reduce_fusion, bf16[256,896]{1,0:T(8,128)(2,1)} %param.6, s32[]{:T(128)S(6)} %select_n.58), kind=kOutput, calls=%fused_computation.13 | convolution fusion | flops 176848896 | bytes 1149956 | tf_op jit(solution)/shard_map/dot_general | solution.py:62
  40.3 2.3 %copy.35 = bf16[768,448]{1,0:T(8,128)(2,1)} copy(bf16[768,448]{0,1:T(8,128)(2,1)} %fusion.3) | data formatting | bytes 1376256 | tf_op jit(solution)/shard_map/convert_element_type | solution.py:65
  42.6 2.3 %reshape.81 = bf16[64,12,448]{2,1,0:T(8,128)(2,1)} reshape(bf16[768,448]{1,0:T(8,128)(2,1)} %copy.35) | data formatting | bytes 1376256 | tf_op jit(solution)/shard_map/reshape | solution.py:66
  44.9 19.8 %all-to-all-done = bf16[64,12,448]{2,1,0:T(8,128)(2,1)S(1)} async-done(((bf16[64,12,448]{2,1,0:T(8,128)(2,1)}), bf16[64,12,448]{2,1,0:T(8,128)(2,1)S(1)}, u32[]{:S(2)}, u32[]{:S(2)}) %all-to-all-start) | async-done | bytes 688160 | tf_op jit(solution)/shard_map/all_to_all | solution.py:67
  64.7 9.1 %all-to-all-start.1 = ((bf16[64,12,448]{2,1,0:T(8,128)(2,1)}), bf16[64,12,448]{2,1,0:T(8,128)(2,1)}, u32[]{:S(2)}, u32[]{:S(2)}) async-start(bf16[64,12,448]{2,1,0:T(8,128)(2,1)} %reshape.81), calls=%async_computation.1 | async-start | bytes 2097152 | tf_op jit(solution)/shard_map/all_to_all | solution.py:67
  73.9 0.8 fusion.24
  74.8 1.3 reshape.80
  76.0 24.3 %all-to-all-done.1 = bf16[64,12,448]{2,1,0:T(8,128)(2,1)} async-done(((bf16[64,12,448]{2,1,0:T(8,128)(2,1)}), bf16[64,12,448]{2,1,0:T(8,128)(2,1)}, u32[]{:S(2)}, u32[]{:S(2)}) %all-to-all-start.1) | async-done | bytes 688160 | tf_op jit(solution)/shard_map/all_to_all | solution.py:67
  100.3 2.3 %reshape.82 = bf16[768,448]{1,0:T(8,128)(2,1)} reshape(bf16[64,12,448]{2,1,0:T(8,128)(2,1)} %all-to-all-done.1) | data formatting | bytes 1376256 | tf_op jit(solution)/shard_map/reshape | solution.py:68
  102.6 1.1 fusion.6
  103.7 1.1 add_convert_fusion
  104.8 0.9 dynamic-slice_bitcast_fusion
  105.8 6.0 %collective-permute-start = (bf16[4,128,768]{2,1,0:T(8,128)(2,1)}, bf16[4,128,768]{2,1,0:T(8,128)(2,1)}, u32[]{:S(2)}, u32[]{:S(2)}) collective-permute-start(bf16[4,128,768]{2,1,0:T(8,128)(2,1)} %dynamic-slice_bitcast_fusion), channel_id=1, source_target_pairs={{0,2},{2,0},{4,6},{6,4},{8,10},{10,8},{12,14},{14,12},{1,3},{3,1},... | collective-permute-start | bytes 2359304 | tf_op jit(solution)/shard_map/ppermute | solution.py:18
  111.8 2.2 %collective-permute-done = bf16[4,128,768]{2,1,0:T(8,128)(2,1)} collective-permute-done((bf16[4,128,768]{2,1,0:T(8,128)(2,1)}, bf16[4,128,768]{2,1,0:T(8,128)(2,1)}, u32[]{:S(2)}, u32[]{:S(2)}) %collective-permute-start) | collective-permute-done | bytes 786464 | tf_op jit(solution)/shard_map/ppermute | solution.py:18
  114.0 1.3 fusion
  115.3 0.9 copy-done.3
  116.2 0.8 dynamic-slice_bitcast_fusion.1
  117.0 3.3 %collective-permute-start.1 = (bf16[2,128,768]{2,1,0:T(8,128)(2,1)}, bf16[2,128,768]{2,1,0:T(8,128)(2,1)}, u32[]{:S(2)}, u32[]{:S(2)}) collective-permute-start(bf16[2,128,768]{2,1,0:T(8,128)(2,1)} %dynamic-slice_bitcast_fusion.1), channel_id=1, source_target_pairs={{0,4},{2,6},{4,0},{6,2},{8,12},{10,14},{12,8},{14,10},{1,5},{3,7},... | collective-permute-start | bytes 1179656 | tf_op jit(solution)/shard_map/ppermute | solution.py:18
  120.2 1.6 all-gather.2.cloned.1.call-done
  121.8 3.7 %convolution_convert_fusion = bf16[448,1024]{1,0:T(8,128)(2,1)} fusion(bf16[768,448]{1,0:T(8,128)(2,1)} %reshape.80, bf16[1024,768]{1,0:T(8,128)(2,1)} %all-gather.2.cloned.1.call-done), kind=kOutput, calls=%fused_computation.8 | convolution fusion | flops 705101824 | bytes 3178496 | tf_op jit(solution)/shard_map/dot_general | solution.py:74
  125.5 4.8 %collective-permute-start.3 = (bf16[448,1024]{1,0:T(8,128)(2,1)}, bf16[448,1024]{1,0:T(8,128)(2,1)}, u32[]{:S(2)}, u32[]{:S(2)}) collective-permute-start(bf16[448,1024]{1,0:T(8,128)(2,1)} %convolution_convert_fusion), channel_id=1, source_target_pairs={{0,1},{1,0},{2,3},{3,2},{4,5},{5,4},{6,7},{7,6},{8,9},{9,8},{10,11... | collective-permute-start | bytes 2752520 | tf_op jit(solution)/shard_map/ppermute | solution.py:77
  130.4 1.1 fusion.10
  131.5 0.7 copy-done.5
  132.3 3.3 %collective-permute-start.2 = (bf16[1,128,768]{2,1,0:T(8,128)(2,1)S(1)}, bf16[1,128,768]{2,1,0:T(8,128)(2,1)S(1)}, u32[]{:S(2)}, u32[]{:S(2)}) collective-permute-start(bf16[1,128,768]{2,1,0:T(8,128)(2,1)S(1)} %constant_dynamic-slice_fusion), channel_id=1, source_target_pairs={{0,8},{2,10},{4,12},{6,14},{8,0},{10,2},{12,4},{14,6},{1,9},{3,11}... | collective-permute-start | bytes 589832 | tf_op jit(solution)/shard_map/ppermute | solution.py:18
  135.6 46.2 %collective-permute-done.2 = bf16[1,128,768]{2,1,0:T(8,128)(2,1)S(1)} collective-permute-done((bf16[1,128,768]{2,1,0:T(8,128)(2,1)S(1)}, bf16[1,128,768]{2,1,0:T(8,128)(2,1)S(1)}, u32[]{:S(2)}, u32[]{:S(2)}) %collective-permute-start.2) | collective-permute-done | bytes 196640 | tf_op jit(solution)/shard_map/ppermute | solution.py:18
  181.8 2.1 %fusion.22 = (bf16[1,1,128,768]{3,2,1,0:T(8,128)(2,1)}, bf16[1,1,128,768]{3,2,1,0:T(8,128)(2,1)}) fusion(bf16[1,1,128,768]{3,2,1,0:T(8,128)(2,1)} %param.10, bf16[1,128,768]{2,1,0:T(8,128)(2,1)S(1)} %collective-permute-done.2, bf16[2,128,768]{2,1,0:T(8,128)(2,1)} %copy-done.5, s32[]{:T(128)S(6)} %select_n.68, bf16[1,1,128,768]{3,2,1,0:T(8,128)(2,1)} %param.11), kind=kLoop, calls=%fused_computation.39 | loop fusion | flops 1769472 | bytes 1179652 | tf_op jit(solution)/shard_map/convert_element_type | solution.py:96
  183.9 3.7 %fusion.4 = bf16[1,448,1024]{2,1,0:T(8,128)(2,1)} fusion(bf16[448,1024]{1,0:T(8,128)(2,1)} %collective-permute-done.3, bf16[768,448]{1,0:T(8,128)(2,1)S(1)} %copy-done.2, bf16[1024,768]{1,0:T(8,128)(2,1)} %all-gather.2.cloned.1.call-done), kind=kOutput, calls=%fused_computation.14 | convolution fusion | flops 706936832 | bytes 4096000 | tf_op jit(solution)/shard_map/dot_general | solution.py:98
  (41 shorter events, 2.6 us)
Async XLA Ops:
  7.2 95.4 %copy-start = (bf16[1,896,1024]{2,1,0:T(8,128)(2,1)S(1)}, bf16[1,896,1024]{2,1,0:T(8,128)(2,1)}, u32[]{:S(2)}) copy-start(bf16[1,896,1024]{2,1,0:T(8,128)(2,1)} %param.9) | copy-start | bytes 5505028
  7.2 4.1 %copy-start.9 = (s32[256,2]{0,1:T(2,128)S(1)}, s32[256,2]{0,1:T(2,128)}, u32[]{:S(2)}) copy-start(s32[256,2]{0,1:T(2,128)} %param.8) | copy-start | bytes 6148
  7.2 4.6 %copy-start.10 = (bf16[256,896]{1,0:T(8,128)(2,1)S(1)}, bf16[256,896]{1,0:T(8,128)(2,1)}, u32[]{:S(2)}) copy-start(bf16[256,896]{1,0:T(8,128)(2,1)} %param.6) | copy-start | bytes 1376260
  13.9 50.8 %all-to-all-start = ((bf16[64,12,448]{2,1,0:T(8,128)(2,1)}), bf16[64,12,448]{2,1,0:T(8,128)(2,1)S(1)}, u32[]{:S(2)}, u32[]{:S(2)}) async-start(bf16[64,12,448]{2,1,0:T(8,128)(2,1)} %reshape.79), calls=%async_computation | async-start | bytes 2097152 | tf_op jit(solution)/shard_map/all_to_all | solution.py:67
  42.6 31.3 %copy-start.7 = (bf16[1,1,128,768]{3,2,1,0:T(8,128)(2,1)S(1)}, bf16[1,1,128,768]{3,2,1,0:T(8,128)(2,1)}, u32[]{:S(2)}) copy-start(bf16[1,1,128,768]{3,2,1,0:T(8,128)(2,1)} %param.10) | copy-start | bytes 589828
  42.6 31.3 %copy-start.8 = (bf16[1,1,128,768]{3,2,1,0:T(8,128)(2,1)S(1)}, bf16[1,1,128,768]{3,2,1,0:T(8,128)(2,1)}, u32[]{:S(2)}) copy-start(bf16[1,1,128,768]{3,2,1,0:T(8,128)(2,1)} %param.11) | copy-start | bytes 589828
  64.7 35.6 %all-to-all-start.1 = ((bf16[64,12,448]{2,1,0:T(8,128)(2,1)}), bf16[64,12,448]{2,1,0:T(8,128)(2,1)}, u32[]{:S(2)}, u32[]{:S(2)}) async-start(bf16[64,12,448]{2,1,0:T(8,128)(2,1)} %reshape.81), calls=%async_computation.1 | async-start | bytes 2097152 | tf_op jit(solution)/shard_map/all_to_all | solution.py:67
  73.8 48.0 %all-gather.2.cloned.1.call-start = ((), (), s32[]{:S(2)}) async-start(), calls=%async_computation.2 | async-start | bytes 1769472 | tf_op jit(solution)/shard_map/all_gather | solution.py:42
  76.0 26.5 %copy-start.6 = (bf16[768,448]{1,0:T(8,128)(2,1)S(1)}, bf16[768,448]{1,0:T(8,128)(2,1)}, u32[]{:S(2)}) copy-start(bf16[768,448]{1,0:T(8,128)(2,1)} %reshape.80) | copy-start | bytes 2064388
  102.6 1.1 copy-start.1
  105.8 8.2 %collective-permute-start = (bf16[4,128,768]{2,1,0:T(8,128)(2,1)}, bf16[4,128,768]{2,1,0:T(8,128)(2,1)}, u32[]{:S(2)}, u32[]{:S(2)}) collective-permute-start(bf16[4,128,768]{2,1,0:T(8,128)(2,1)} %dynamic-slice_bitcast_fusion), channel_id=1, source_target_pairs={{0,2},{2,0},{4,6},{6,4},{8,10},{10,8},{12,14},{14,12},{1,3},{3,1},... | collective-permute-start | bytes 2359304 | tf_op jit(solution)/shard_map/ppermute | solution.py:18
  115.3 0.9 copy-start.3
  117.0 13.5 %copy-start.4 = (bf16[4,128,768]{2,1,0:T(8,128)(2,1)S(1)}, bf16[4,128,768]{2,1,0:T(8,128)(2,1)}, u32[]{:S(2)}) copy-start(bf16[4,128,768]{2,1,0:T(8,128)(2,1)} %copy-done.3) | copy-start | bytes 2359300
  117.0 13.4 %collective-permute-start.1 = (bf16[2,128,768]{2,1,0:T(8,128)(2,1)}, bf16[2,128,768]{2,1,0:T(8,128)(2,1)}, u32[]{:S(2)}, u32[]{:S(2)}) collective-permute-start(bf16[2,128,768]{2,1,0:T(8,128)(2,1)} %dynamic-slice_bitcast_fusion.1), channel_id=1, source_target_pairs={{0,4},{2,6},{4,0},{6,2},{8,12},{10,14},{12,8},{14,10},{1,5},{3,7},... | collective-permute-start | bytes 1179656 | tf_op jit(solution)/shard_map/ppermute | solution.py:18
  125.5 58.4 %copy-start.2 = (bf16[768,448]{1,0:T(8,128)(2,1)S(1)}, bf16[768,448]{1,0:T(8,128)(2,1)}, u32[]{:S(2)}) copy-start(bf16[768,448]{1,0:T(8,128)(2,1)} %reshape.82) | copy-start | bytes 2064388
  125.5 58.4 %collective-permute-start.3 = (bf16[448,1024]{1,0:T(8,128)(2,1)}, bf16[448,1024]{1,0:T(8,128)(2,1)}, u32[]{:S(2)}, u32[]{:S(2)}) collective-permute-start(bf16[448,1024]{1,0:T(8,128)(2,1)} %convolution_convert_fusion), channel_id=1, source_target_pairs={{0,1},{1,0},{2,3},{3,2},{4,5},{5,4},{6,7},{7,6},{8,9},{9,8},{10,11... | collective-permute-start | bytes 2752520 | tf_op jit(solution)/shard_map/ppermute | solution.py:77
  131.5 0.8 copy-start.5
  132.3 49.5 %collective-permute-start.2 = (bf16[1,128,768]{2,1,0:T(8,128)(2,1)S(1)}, bf16[1,128,768]{2,1,0:T(8,128)(2,1)S(1)}, u32[]{:S(2)}, u32[]{:S(2)}) collective-permute-start(bf16[1,128,768]{2,1,0:T(8,128)(2,1)S(1)} %constant_dynamic-slice_fusion), channel_id=1, source_target_pairs={{0,8},{2,10},{4,12},{6,14},{8,0},{10,2},{12,4},{14,6},{1,9},{3,11}... | collective-permute-start | bytes 589832 | tf_op jit(solution)/shard_map/ppermute | solution.py:18
Sparse Core Ops, SparseCore 0:
  77.9 43.8 all-gather.1

commit v6 on v2

--- a/solution.py
+++ b/solution.py
@@ -2,6 +2,26 @@
 import jax.numpy as jnp
 from jax import lax
 from jax.sharding import PartitionSpec as P
+
+
+def scatter_sum_et(part):
+    et_count = lax.axis_size("et")
+    et_index = lax.axis_index("et")
+    chips = et_count // 2
+    chip = et_index // 2
+    rows = part.shape[0] // et_count
+    groups = part.reshape(chips, 2, rows, part.shape[1])
+    core = et_index % 2
+    keep = lax.dynamic_index_in_dim(groups, core, axis=1, keepdims=False)
+    away = lax.dynamic_index_in_dim(groups, 1 - core, axis=1, keepdims=False)
+    got = lax.ppermute(away, "et", [(i, i ^ 1) for i in range(et_count)])
+    chip_sum = (keep.astype(jnp.float32) + got.astype(jnp.float32)).astype(jnp.bfloat16)
+    total = lax.dynamic_index_in_dim(chip_sum, chip, axis=0, keepdims=False).astype(jnp.float32)
+    for shift in range(1, chips):
+        block = lax.dynamic_index_in_dim(chip_sum, (chip + shift) % chips, axis=0, keepdims=False)
+        pairs = [(i, ((i // 2 + shift) % chips) * 2 + i % 2) for i in range(et_count)]
+        total = total + lax.ppermute(block, "et", pairs).astype(jnp.float32)
+    return total
 
 
 def local(grad_out, combine, routing, expert_down_matrix, gate_pre, up_pre):
@@ -69,12 +89,7 @@
         (((0,), (1,)), ((), ())),
         preferred_element_type=jnp.float32,
     )
-    act_grad = lax.psum_scatter(
-        block_sum.astype(jnp.bfloat16),
-        "et",
-        scatter_dimension=0,
-        tiled=True,
-    ).astype(jnp.float32)
+    act_grad = scatter_sum_et(block_sum.astype(jnp.bfloat16))
     grad_gate = (
         act_grad * up_vals * gate_sig * (1.0 + gate_activation_values * (1.0 - gate_sig))
     ).astype(jnp.bfloat16)

time: 182 us -> 193 us (1.060)
  the two profiles are of different devices: /device:TPU:56 before, /device:TPU:39 now
where the time goes in v6:
time: 193 us; the launch traced here: 192 us
  waiting for transfers between devices  95.4 us (49%)
  starting transfers between devices  49.9 us (26%)
  between operations  14.4 us (7%)
  local copies, waits for them, and re-layouts  14.2 us (7%)
  matrix products  12.2 us (6%)
  other arithmetic  6.34 us (3%)
    ppermute x3, waiting for transfers between devices, scatter_sum_et(): total = total + lax.ppermute(block, 'et', pairs).astype(jnp.float32)  48.8 us
    all_to_all x2, waiting for transfers between devices, routed(): sent = lax.all_to_all(rows, 'ep', split_axis=0, concat_axis=0, tiled=True)  46.5 us
    all_to_all x2, starting transfers between devices, routed(): sent = lax.all_to_all(rows, 'ep', split_axis=0, concat_axis=0, tiled=True)  30.4 us
    ppermute x3, starting transfers between devices, scatter_sum_et(): total = total + lax.ppermute(block, 'et', pairs).astype(jnp.float32)  9.35 us
    ppermute x1, starting transfers between devices, scatter_sum_et(): got = lax.ppermute(away, 'et', [(i, i ^ 1) for i in range(et_count)])  5.74 us
    ppermute x1, starting transfers between devices, local(): received = lax.ppermute(away_part, 'rep', [(0, 1), (1, 0)])  4.39 us
  transfers between devices with their start and end apart: 8, of which 4 were waited for; matrix products, arithmetic and copies ran while one was open for 11% of the time, Pallas kernels for 0%

profile of v6, /device:TPU:39, one launch (start us, length us, event | category | flops | bytes accessed | tf_op | source)
XLA Modules:
  0.0 192.5 jit_solution(9629602544178792351)
XLA Ops:
  7.2 1.0 copy.30
  8.5 1.2 reduce-window.6
  10.3 0.8 copy.34
  11.3 0.3 fusion.1
  11.8 0.6 fusion.2
  12.4 0.3 copy.35
  12.7 1.2 reshape.74
  14.0 22.5 %all-to-all-start = ((bf16[64,12,448]{2,1,0:T(8,128)(2,1)}), bf16[64,12,448]{2,1,0:T(8,128)(2,1)S(1)}, u32[]{:S(2)}, u32[]{:S(2)}) async-start(bf16[64,12,448]{2,1,0:T(8,128)(2,1)} %reshape.74), calls=%async_computation | async-start | bytes 2097152 | tf_op jit(solution)/shard_map/all_to_all | solution.py:67
  36.5 0.8 fusion.25
  37.4 2.4 %fusion.3 = bf16[768,448]{0,1:T(8,128)(2,1)} fusion(pred[768,256]{1,0:T(8,128)(4,1)S(1)} %fusion.1, f32[768]{0:T(1024)S(1)} %select_reduce_fusion, bf16[256,896]{1,0:T(8,128)(2,1)} %param.6, s32[]{:T(128)S(6)} %select_n.57), kind=kOutput, calls=%fused_computation.13 | convolution fusion | flops 176848896 | bytes 1149956 | tf_op jit(solution)/shard_map/dot_general | solution.py:62
  39.8 2.3 %copy.36 = bf16[768,448]{1,0:T(8,128)(2,1)} copy(bf16[768,448]{0,1:T(8,128)(2,1)} %fusion.3) | data formatting | bytes 1376256 | tf_op jit(solution)/shard_map/convert_element_type | solution.py:65
  42.0 2.3 %reshape.76 = bf16[64,12,448]{2,1,0:T(8,128)(2,1)} reshape(bf16[768,448]{1,0:T(8,128)(2,1)} %copy.36) | data formatting | bytes 1376256 | tf_op jit(solution)/shard_map/reshape | solution.py:66
  44.3 20.1 %all-to-all-done = bf16[64,12,448]{2,1,0:T(8,128)(2,1)S(1)} async-done(((bf16[64,12,448]{2,1,0:T(8,128)(2,1)}), bf16[64,12,448]{2,1,0:T(8,128)(2,1)S(1)}, u32[]{:S(2)}, u32[]{:S(2)}) %all-to-all-start) | async-done | bytes 688160 | tf_op jit(solution)/shard_map/all_to_all | solution.py:67
  64.4 7.9 %all-to-all-start.1 = ((bf16[64,12,448]{2,1,0:T(8,128)(2,1)}), bf16[64,12,448]{2,1,0:T(8,128)(2,1)}, u32[]{:S(2)}, u32[]{:S(2)}) async-start(bf16[64,12,448]{2,1,0:T(8,128)(2,1)} %reshape.76), calls=%async_computation.1 | async-start | bytes 2097152 | tf_op jit(solution)/shard_map/all_to_all | solution.py:67
  72.4 1.3 reshape.75
  73.7 26.4 %all-to-all-done.1 = bf16[64,12,448]{2,1,0:T(8,128)(2,1)} async-done(((bf16[64,12,448]{2,1,0:T(8,128)(2,1)}), bf16[64,12,448]{2,1,0:T(8,128)(2,1)}, u32[]{:S(2)}, u32[]{:S(2)}) %all-to-all-start.1) | async-done | bytes 688160 | tf_op jit(solution)/shard_map/all_to_all | solution.py:67
  100.1 2.3 %reshape.77 = bf16[768,448]{1,0:T(8,128)(2,1)} reshape(bf16[64,12,448]{2,1,0:T(8,128)(2,1)} %all-to-all-done.1) | data formatting | bytes 1376256 | tf_op jit(solution)/shard_map/reshape | solution.py:68
  102.3 1.1 fusion.6
  103.5 1.1 add_convert_fusion
  104.6 1.0 dynamic-slice_bitcast_fusion
  105.5 5.7 %collective-permute-start = (bf16[4,128,768]{2,1,0:T(8,128)(2,1)}, bf16[4,128,768]{2,1,0:T(8,128)(2,1)}, u32[]{:S(2)}, u32[]{:S(2)}) collective-permute-start(bf16[4,128,768]{2,1,0:T(8,128)(2,1)} %dynamic-slice_bitcast_fusion), channel_id=1, source_target_pairs={{0,2},{2,0},{4,6},{6,4},{8,10},{10,8},{12,14},{14,12},{1,3},{3,1},... | collective-permute-start | bytes 2359304 | tf_op jit(solution)/shard_map/ppermute | solution.py:17
  111.3 3.7 %convolution_convert_fusion = bf16[448,1024]{1,0:T(8,128)(2,1)} fusion(bf16[768,448]{1,0:T(8,128)(2,1)} %reshape.75, bf16[1024,768]{1,0:T(8,128)(2,1)} %all-gather.2.cloned.1.call-done), kind=kOutput, calls=%fused_computation.8 | convolution fusion | flops 705101824 | bytes 3178496 | tf_op jit(solution)/shard_map/dot_general | solution.py:74
  115.0 4.4 %collective-permute-start.4 = (bf16[448,1024]{1,0:T(8,128)(2,1)}, bf16[448,1024]{1,0:T(8,128)(2,1)}, u32[]{:S(2)}, u32[]{:S(2)}) collective-permute-start(bf16[448,1024]{1,0:T(8,128)(2,1)} %convolution_convert_fusion), channel_id=1, source_target_pairs={{0,1},{1,0},{2,3},{3,2},{4,5},{5,4},{6,7},{7,6},{8,9},{9,8},{10,11... | collective-permute-start | bytes 2752520 | tf_op jit(solution)/shard_map/ppermute | solution.py:77
  119.5 1.3 fusion
  120.9 0.9 copy-done.3
  121.8 5.0 %collective-permute-start.1 = (bf16[128,768]{1,0:T(8,128)(2,1)S(1)}, bf16[128,768]{1,0:T(8,128)(2,1)S(1)}, u32[]{:S(2)}, u32[]{:S(2)}) collective-permute-start(bf16[128,768]{1,0:T(8,128)(2,1)S(1)} %get-tuple-element.11), channel_id=1, source_target_pairs={{0,4},{2,6},{4,8},{6,10},{8,12},{10,14},{12,0},{14,2},{1,5},{3,7},... | collective-permute-start | bytes 589832 | tf_op jit(solution)/shard_map/ppermute | solution.py:23
  126.8 1.9 collective-permute-start.2
  128.7 2.4 %collective-permute-start.3 = (bf16[128,768]{1,0:T(8,128)(2,1)S(1)}, bf16[128,768]{1,0:T(8,128)(2,1)}, u32[]{:S(2)}, u32[]{:S(2)}) collective-permute-start(bf16[128,768]{1,0:T(8,128)(2,1)S(1)} %get-tuple-element.12), channel_id=1, source_target_pairs={{0,12},{2,14},{4,0},{6,2},{8,4},{10,6},{12,8},{14,10},{1,13},{3,15... | collective-permute-start | bytes 589832 | tf_op jit(solution)/shard_map/ppermute | solution.py:23
  131.2 34.0 %collective-permute-done.1 = bf16[128,768]{1,0:T(8,128)(2,1)S(1)} collective-permute-done((bf16[128,768]{1,0:T(8,128)(2,1)S(1)}, bf16[128,768]{1,0:T(8,128)(2,1)S(1)}, u32[]{:S(2)}, u32[]{:S(2)}) %collective-permute-start.1) | collective-permute-done | bytes 196640 | tf_op jit(solution)/shard_map/ppermute | solution.py:23
  165.2 14.8 %collective-permute-done.2 = bf16[128,768]{1,0:T(8,128)(2,1)} collective-permute-done((bf16[128,768]{1,0:T(8,128)(2,1)S(1)}, bf16[128,768]{1,0:T(8,128)(2,1)}, u32[]{:S(2)}, u32[]{:S(2)}) %collective-permute-start.2) | collective-permute-done | bytes 196640 | tf_op jit(solution)/shard_map/ppermute | solution.py:23
  180.0 2.3 %fusion.28 = (bf16[1,1,128,768]{3,2,1,0:T(8,128)(2,1)}, bf16[1,1,128,768]{3,2,1,0:T(8,128)(2,1)}) fusion(bf16[1,1,128,768]{3,2,1,0:T(8,128)(2,1)} %param.10, bf16[128,768]{1,0:T(8,128)(2,1)} %collective-permute-done.3, bf16[128,768]{1,0:T(8,128)(2,1)} %collective-permute-done.2, bf16[128,768]{1,0:T(8,128)(2,1)S(1)} %collective-permute-done.1, ...), kind=kLoop, calls=%fused_computation.49 | loop fusion | flops 2162688 | bytes 1572868 | tf_op jit(solution)/shard_map/broadcast_in_dim | solution.py:102
  182.3 3.3 %fusion.4 = bf16[1,448,1024]{2,1,0:T(8,128)(2,1)} fusion(bf16[448,1024]{1,0:T(8,128)(2,1)} %collective-permute-done.4, bf16[768,448]{1,0:T(8,128)(2,1)S(1)} %copy-done.2, bf16[1024,768]{1,0:T(8,128)(2,1)S(1)} %copy-done.8), kind=kOutput, calls=%fused_computation.14 | convolution fusion | flops 706936832 | bytes 4096000 | tf_op jit(solution)/shard_map/dot_general | solution.py:98
  (39 shorter events, 1.5 us)
Async XLA Ops:
  7.2 95.2 %copy-start = (bf16[1,896,1024]{2,1,0:T(8,128)(2,1)S(1)}, bf16[1,896,1024]{2,1,0:T(8,128)(2,1)}, u32[]{:S(2)}) copy-start(bf16[1,896,1024]{2,1,0:T(8,128)(2,1)} %param.9) | copy-start | bytes 5505028
  7.2 4.1 %copy-start.7 = (s32[256,2]{0,1:T(2,128)S(1)}, s32[256,2]{0,1:T(2,128)}, u32[]{:S(2)}) copy-start(s32[256,2]{0,1:T(2,128)} %param.8) | copy-start | bytes 6148
  7.2 4.6 %copy-start.9 = (bf16[256,896]{1,0:T(8,128)(2,1)S(1)}, bf16[256,896]{1,0:T(8,128)(2,1)}, u32[]{:S(2)}) copy-start(bf16[256,896]{1,0:T(8,128)(2,1)} %param.6) | copy-start | bytes 1376260
  12.7 23.8 %copy-start.5 = (bf16[1,1,128,768]{3,2,1,0:T(8,128)(2,1)S(1)}, bf16[1,1,128,768]{3,2,1,0:T(8,128)(2,1)}, u32[]{:S(2)}) copy-start(bf16[1,1,128,768]{3,2,1,0:T(8,128)(2,1)} %param.10) | copy-start | bytes 589828
  12.7 23.8 %copy-start.6 = (bf16[1,1,128,768]{3,2,1,0:T(8,128)(2,1)S(1)}, bf16[1,1,128,768]{3,2,1,0:T(8,128)(2,1)}, u32[]{:S(2)}) copy-start(bf16[1,1,128,768]{3,2,1,0:T(8,128)(2,1)} %param.11) | copy-start | bytes 589828
  14.0 50.5 %all-to-all-start = ((bf16[64,12,448]{2,1,0:T(8,128)(2,1)}), bf16[64,12,448]{2,1,0:T(8,128)(2,1)S(1)}, u32[]{:S(2)}, u32[]{:S(2)}) async-start(bf16[64,12,448]{2,1,0:T(8,128)(2,1)} %reshape.74), calls=%async_computation | async-start | bytes 2097152 | tf_op jit(solution)/shard_map/all_to_all | solution.py:67
  36.5 74.8 %all-gather.2.cloned.1.call-start = ((), (), s32[]{:S(2)}) async-start(), calls=%async_computation.2 | async-start | bytes 1769472 | tf_op jit(solution)/shard_map/all_gather | solution.py:42
  64.4 35.6 %all-to-all-start.1 = ((bf16[64,12,448]{2,1,0:T(8,128)(2,1)}), bf16[64,12,448]{2,1,0:T(8,128)(2,1)}, u32[]{:S(2)}, u32[]{:S(2)}) async-start(bf16[64,12,448]{2,1,0:T(8,128)(2,1)} %reshape.76), calls=%async_computation.1 | async-start | bytes 2097152 | tf_op jit(solution)/shard_map/all_to_all | solution.py:67
  73.7 28.7 %copy-start.4 = (bf16[768,448]{1,0:T(8,128)(2,1)S(1)}, bf16[768,448]{1,0:T(8,128)(2,1)}, u32[]{:S(2)}) copy-start(bf16[768,448]{1,0:T(8,128)(2,1)} %reshape.75) | copy-start | bytes 2064388
  102.3 1.1 copy-start.1
  105.5 14.0 %collective-permute-start = (bf16[4,128,768]{2,1,0:T(8,128)(2,1)}, bf16[4,128,768]{2,1,0:T(8,128)(2,1)}, u32[]{:S(2)}, u32[]{:S(2)}) collective-permute-start(bf16[4,128,768]{2,1,0:T(8,128)(2,1)} %dynamic-slice_bitcast_fusion), channel_id=1, source_target_pairs={{0,2},{2,0},{4,6},{6,4},{8,10},{10,8},{12,14},{14,12},{1,3},{3,1},... | collective-permute-start | bytes 2359304 | tf_op jit(solution)/shard_map/ppermute | solution.py:17
  115.0 67.3 %collective-permute-start.4 = (bf16[448,1024]{1,0:T(8,128)(2,1)}, bf16[448,1024]{1,0:T(8,128)(2,1)}, u32[]{:S(2)}, u32[]{:S(2)}) collective-permute-start(bf16[448,1024]{1,0:T(8,128)(2,1)} %convolution_convert_fusion), channel_id=1, source_target_pairs={{0,1},{1,0},{2,3},{3,2},{4,5},{5,4},{6,7},{7,6},{8,9},{9,8},{10,11... | collective-permute-start | bytes 2752520 | tf_op jit(solution)/shard_map/ppermute | solution.py:77
  120.9 0.9 copy-start.3
  121.8 60.6 %copy-start.2 = (bf16[768,448]{1,0:T(8,128)(2,1)S(1)}, bf16[768,448]{1,0:T(8,128)(2,1)}, u32[]{:S(2)}) copy-start(bf16[768,448]{1,0:T(8,128)(2,1)} %reshape.77) | copy-start | bytes 2064388
  121.8 43.4 %collective-permute-start.1 = (bf16[128,768]{1,0:T(8,128)(2,1)S(1)}, bf16[128,768]{1,0:T(8,128)(2,1)S(1)}, u32[]{:S(2)}, u32[]{:S(2)}) collective-permute-start(bf16[128,768]{1,0:T(8,128)(2,1)S(1)} %get-tuple-element.11), channel_id=1, source_target_pairs={{0,4},{2,6},{4,8},{6,10},{8,12},{10,14},{12,0},{14,2},{1,5},{3,7},... | collective-permute-start | bytes 589832 | tf_op jit(solution)/shard_map/ppermute | solution.py:23
  126.8 53.2 %collective-permute-start.2 = (bf16[128,768]{1,0:T(8,128)(2,1)S(1)}, bf16[128,768]{1,0:T(8,128)(2,1)}, u32[]{:S(2)}, u32[]{:S(2)}) collective-permute-start(bf16[128,768]{1,0:T(8,128)(2,1)S(1)} %get-tuple-element.13), channel_id=1, source_target_pairs={{0,8},{2,10},{4,12},{6,14},{8,0},{10,2},{12,4},{14,6},{1,9},{3,11}... | collective-permute-start | bytes 589832 | tf_op jit(solution)/shard_map/ppermute | solution.py:23
  128.7 51.3 %collective-permute-start.3 = (bf16[128,768]{1,0:T(8,128)(2,1)S(1)}, bf16[128,768]{1,0:T(8,128)(2,1)}, u32[]{:S(2)}, u32[]{:S(2)}) collective-permute-start(bf16[128,768]{1,0:T(8,128)(2,1)S(1)} %get-tuple-element.12), channel_id=1, source_target_pairs={{0,12},{2,14},{4,0},{6,2},{8,4},{10,6},{12,8},{14,10},{1,13},{3,15... | collective-permute-start | bytes 589832 | tf_op jit(solution)/shard_map/ppermute | solution.py:23
  131.2 51.2 %copy-start.8 = (bf16[1024,768]{1,0:T(8,128)(2,1)S(1)}, bf16[1024,768]{1,0:T(8,128)(2,1)}, u32[]{:S(2)}) copy-start(bf16[1024,768]{1,0:T(8,128)(2,1)} %all-gather.2.cloned.1.call-done) | copy-start | bytes 4718596
Sparse Core Ops, SparseCore 0:
  40.5 42.8 all-gather.1
